TPU v7x, 256 devices: a whole 4x4x8 slice. The times are simulated.
256 devices in a mesh: chan: 64 (over z, y_lo, x), ma: 4 (over y_hi, core).
Axes of the slice: x: 4, y: 4 (y_hi: 2, y_lo: 2; y = y_hi * 2 + y_lo), z: 8, core: 2. Of those that a mesh axis runs over, the one named last changes fastest.
Arguments:
- beam_table: bfloat16 [512, 1024, 2048], P(('ma', 'chan')), parts along dimension 0, may hold values from -0.125 to 0.125
- covariance: bfloat16 [8192, 128, 128], P(('ma', 'chan')), parts along dimension 0, as said below
- noise_var: float32 [512, 512], P(('ma', 'chan')), parts along dimension 0, may hold values from 0.5 to 4
- start_field: float32 [512, 512, 256], P(('ma', 'chan')), parts along dimension 0, may hold values from -4 to 4
- probes: float32 [512, 512, 256], P(('ma', 'chan')), parts along dimension 0, may hold values from -6 to 6
Outputs:
- solved: float32 [512, 512, 256], P(('ma', 'chan')), parts along dimension 0
- multipole_band_power: bfloat16 [8192, 128, 128], P(('ma', 'chan')), parts along dimension 0
There are 4 independent parts, one for each index of `ma`. A program takes and returns all parts, laid end to end along the dimension named above; each array names one. Nothing has to cross between parts.
Inputs may be any that keep to these rules, and one draw needn't show every extreme that they name: Each covariance[l] is symmetric with diagonal entries between 1 and 2.
All inputs are finite; a program needn't handle non-finite values.
Results may differ from a plain program's by a relative error of at most 0.009.
Values may be sent and summed in bfloat16 or wider, within the bound.
No kernel may reach another device: no remote copies, remote signals or barrier semaphores. Data moves between devices by JAX's collectives and lax.ppermute only.
A program may use at most 128 MiB of HBM per device.

v0:
```python
import jax
import jax.numpy as jnp
from jax import lax
from jax.sharding import PartitionSpec as P

ITERS = 2


WEIGHT = 0.2


def project_back(beam_table, field_b):
    column_entries = field_b.shape[2] // 2
    reals = field_b[:, :, :column_entries]
    imags = field_b[:, :, column_entries:]
    lower = jnp.concatenate([imags, -reals], axis=2)
    stacked = jnp.concatenate([field_b, lower], axis=1)
    return jnp.einsum("fkl,fkc->flc", beam_table, stacked, preferred_element_type=jnp.float32)


def project_out(beam_table, mixed_back):
    column_entries = mixed_back.shape[2] // 2
    modes = beam_table.shape[1] // 2
    product = jnp.einsum("fkl,flc->fkc", beam_table, mixed_back, preferred_element_type=jnp.float32)
    upper = product[:, :modes]
    lower = product[:, modes:]
    return jnp.concatenate(
        [
            upper[:, :, :column_entries] - lower[:, :, column_entries:],
            upper[:, :, column_entries:] + lower[:, :, :column_entries],
        ],
        axis=2,
    )


def apply_operator(beam_table, covariance, field):
    field_b = field.astype(jnp.bfloat16)
    sky_map = project_back(beam_table, field_b).astype(jnp.bfloat16)
    channel_mixed = jnp.einsum(
        "drj,jdi->rdi",
        covariance,
        lax.all_to_all(sky_map, "chan", split_axis=1, concat_axis=0, tiled=True),
        preferred_element_type=jnp.float32,
    )
    mixed_back = lax.all_to_all(
        channel_mixed.astype(jnp.bfloat16), "chan", split_axis=0, concat_axis=1, tiled=True
    )
    return project_out(beam_table, mixed_back)


def on_device(beam_table, covariance, noise_var, start_field, probes):
    field = start_field
    column_entries = field.shape[2] // 2
    for repeat in range(ITERS):
        image = apply_operator(beam_table, covariance, field)
        field = field + WEIGHT * (probes - image - noise_var[:, :, None] * field)
    final_sky = project_back(beam_table, field.astype(jnp.bfloat16)).astype(jnp.bfloat16)
    collected_parts = lax.all_to_all(final_sky, "chan", split_axis=1, concat_axis=0, tiled=True)
    multipole_band_power = (
        jnp.einsum(
            "mjk,ujk->jmu", collected_parts, collected_parts, preferred_element_type=jnp.float32
        )
        / column_entries
    )
    return (field, multipole_band_power.astype(jnp.bfloat16))


def solution(mesh):
    return jax.shard_map(
        on_device,
        mesh=mesh,
        in_specs=(
            P(("ma", "chan"), None, None),
            P(("ma", "chan"), None, None),
            P(("ma", "chan"), None),
            P(("ma", "chan"), None, None),
            P(("ma", "chan"), None, None),
        ),
        out_specs=(P(("ma", "chan"), None, None), P(("ma", "chan"), None, None)),
        check_vma=False,
    )
```

profile of v0, /device:TPU:2, one launch (start us, length us, event | category | flops | bytes accessed | tf_op | source)
XLA Modules:
  0.0 362.9 jit_solution(1768359897878251081)
XLA Ops:
  0.6 0.0 copy-start
  0.6 1.6 copy.48
  2.3 0.1 convert_element_type.42
  2.4 7.2 %fusion = bf16[2,2048,256]{1,2,0:T(8,128)(2,1)} fusion(bf16[2,1024,2048]{2,1,0:T(8,128)(2,1)} %param.5, bf16[2,512,128]{1,2,0:T(8,128)(2,1)S(1)} %get-tuple-element.19, bf16[2,512,128]{1,2,0:T(8,128)(2,1)S(1)} %get-tuple-element.18, bf16[2,512,256]{1,2,0:T(8,128)(2,1)S(1)} %convert_element_type.42), kind=kOutput, calls=%fused_computation.3 | convolution fusion | flops 2151677952 | bytes 11534336 | tf_op jit(solution)/shard_map/fkl,fkc->flc/dot_general | solution.py:18
  9.6 6.1 %copy.39 = bf16[2,2048,256]{2,0,1:T(2,128)(2,1)} copy(bf16[2,2048,256]{1,2,0:T(8,128)(2,1)} %fusion) | data formatting | bytes 4194304 | tf_op jit(solution)/shard_map/convert_element_type | solution.py:38
  15.7 63.4 %all_to_all.90 = bf16[2,2048,256]{2,0,1:T(2,128)(2,1)S(1)} all-to-all(bf16[2,2048,256]{2,0,1:T(2,128)(2,1)} %copy.39), channel_id=1, replica_groups=mesh['chan'=64,'ma'=4] {'chan'}, dimensions={1} | all-to-all | bytes 4194304 | tf_op jit(solution)/shard_map/all_to_all | solution.py:42
  79.2 0.3 copy.40
  79.4 0.2 copy.41
  79.6 3.0 convert_bitcast_fusion.1
  82.6 4.6 %copy.43 = bf16[128,32,256]{2,1,0:T(8,128)(2,1)} copy(bf16[128,32,256]{0,2,1:T(8,128)(2,1)} %convert_bitcast_fusion.1) | data formatting | bytes 4194304 | tf_op jit(solution)/shard_map/convert_element_type | solution.py:46
  87.2 7.1 %all-to-all-start.1 = ((bf16[128,32,256]{2,1,0:T(8,128)(2,1)}), bf16[128,32,256]{2,1,0:T(8,128)(2,1)}, u32[]{:S(2)}, u32[]{:S(2)}) async-start(bf16[128,32,256]{2,1,0:T(8,128)(2,1)} %copy.43), calls=%async_computation.1 | async-start | bytes 4194304 | tf_op jit(solution)/shard_map/all_to_all | solution.py:45
  94.3 1.6 copy.46
  95.8 47.6 %all-to-all-done.1 = bf16[128,32,256]{2,1,0:T(8,128)(2,1)} async-done(((bf16[128,32,256]{2,1,0:T(8,128)(2,1)}), bf16[128,32,256]{2,1,0:T(8,128)(2,1)}, u32[]{:S(2)}, u32[]{:S(2)}) %all-to-all-start.1) | async-done | bytes 2097184 | tf_op jit(solution)/shard_map/all_to_all | solution.py:45
  143.5 1.9 copy.44
  145.4 0.0 slice-start.1
  145.4 6.2 %convolution_bitcast_fusion.1 = f32[2,1024,256]{1,2,0:T(8,128)S(1)} fusion(bf16[2,2048,256]{2,1,0:T(8,128)(2,1)S(1)} %bitcast.52, bf16[2,1024,2048]{2,1,0:T(8,128)(2,1)} %param.5), kind=kOutput, calls=%fused_computation.14 | convolution fusion | flops 2147483648 | bytes 12582912 | tf_op jit(solution)/shard_map/fkl,flc->fkc/dot_general | solution.py:24
  151.6 0.0 copy-start.7
  151.6 0.2 slice_subtract_fusion.1
  151.9 0.0 copy-start.2
  151.9 0.0 copy-start.4
  151.9 0.4 copy-done.7
  152.3 0.4 fusion.32
  152.8 0.0 copy-done.4
  152.8 3.8 %fusion.1 = bf16[2,2048,256]{1,2,0:T(8,128)(2,1)} fusion(bf16[2,1024,2048]{2,1,0:T(8,128)(2,1)S(1)} %bitcast.55, bf16[2,512,128]{1,2,0:T(8,128)(2,1)S(1)} %get-tuple-element.17, bf16[2,512,128]{1,2,0:T(8,128)(2,1)S(1)} %get-tuple-element.16, bf16[2,512,256]{1,2,0:T(8,128)(2,1)S(1)} %fusion.32), kind=kOutput, calls=%fused_computation.4 | convolution fusion | flops 2151677952 | bytes 11534336 | tf_op jit(solution)/shard_map/fkl,fkc->flc/dot_general | solution.py:18
  156.7 6.1 %copy.49 = bf16[2,2048,256]{2,0,1:T(2,128)(2,1)} copy(bf16[2,2048,256]{1,2,0:T(8,128)(2,1)} %fusion.1) | data formatting | bytes 4194304 | tf_op jit(solution)/shard_map/convert_element_type | solution.py:38
  162.8 56.1 %all_to_all.91 = bf16[2,2048,256]{2,0,1:T(2,128)(2,1)S(1)} all-to-all(bf16[2,2048,256]{2,0,1:T(2,128)(2,1)} %copy.49), channel_id=1, replica_groups=mesh['chan'=64,'ma'=4] {'chan'}, dimensions={1} | all-to-all | bytes 4194304 | tf_op jit(solution)/shard_map/all_to_all | solution.py:42
  218.9 0.3 copy.50
  219.1 0.2 copy.51
  219.3 3.0 convert_bitcast_fusion
  222.3 4.5 %copy.53 = bf16[128,32,256]{2,1,0:T(8,128)(2,1)} copy(bf16[128,32,256]{0,2,1:T(8,128)(2,1)} %convert_bitcast_fusion) | data formatting | bytes 4194304 | tf_op jit(solution)/shard_map/convert_element_type | solution.py:46
  226.9 56.0 %all_to_all.92 = bf16[128,32,256]{2,1,0:T(8,128)(2,1)S(1)} all-to-all(bf16[128,32,256]{2,1,0:T(8,128)(2,1)} %copy.53), channel_id=1, replica_groups=mesh['chan'=64,'ma'=4] {'chan'}, dimensions={0} | all-to-all | bytes 4194304 | tf_op jit(solution)/shard_map/all_to_all | solution.py:45
  282.9 0.2 copy.54
  283.1 0.0 slice-start.3
  283.1 6.2 %convolution_bitcast_fusion = f32[2,1024,256]{1,2,0:T(8,128)S(1)} fusion(bf16[2,2048,256]{2,1,0:T(8,128)(2,1)S(1)} %bitcast.53, bf16[2,1024,2048]{2,1,0:T(8,128)(2,1)} %param.5), kind=kOutput, calls=%fused_computation.13 | convolution fusion | flops 2147483648 | bytes 12582912 | tf_op jit(solution)/shard_map/fkl,flc->fkc/dot_general | solution.py:24
  289.4 0.0 copy-start.5
  289.4 0.2 slice_subtract_fusion
  289.6 0.8 copy-done.3
  290.4 0.2 copy-done.5
  290.6 1.5 fusion.36
  292.1 2.5 fusion.2
  294.6 3.8 %copy.57 = bf16[2,2048,256]{2,0,1:T(2,128)(2,1)} copy(bf16[2,2048,256]{1,2,0:T(8,128)(2,1)S(1)} %fusion.2) | data formatting | bytes 4194304 | tf_op jit(solution)/shard_map/convert_element_type | solution.py:57
  298.5 7.0 %all-to-all-start.4 = ((bf16[2,2048,256]{2,0,1:T(2,128)(2,1)}), bf16[2,2048,256]{2,0,1:T(2,128)(2,1)S(1)}, u32[]{:S(2)}, u32[]{:S(2)}) async-start(bf16[2,2048,256]{2,0,1:T(2,128)(2,1)} %copy.57), calls=%async_computation.4 | async-start | bytes 4194304 | tf_op jit(solution)/shard_map/all_to_all | solution.py:58
  305.5 1.3 copy.60
  306.8 47.8 %all-to-all-done.4 = bf16[2,2048,256]{2,0,1:T(2,128)(2,1)S(1)} async-done(((bf16[2,2048,256]{2,0,1:T(2,128)(2,1)}), bf16[2,2048,256]{2,0,1:T(2,128)(2,1)S(1)}, u32[]{:S(2)}, u32[]{:S(2)}) %all-to-all-start.4) | async-done | bytes 2097184 | tf_op jit(solution)/shard_map/all_to_all | solution.py:58
  354.6 0.3 copy.58
  354.9 3.5 copy.59
  358.4 2.8 all_to_all.84
  361.2 1.7 multiply_convert_fusion
  (18 shorter events, 0.1 us)
Async XLA Ops:
  0.6 79.0 %copy-start = (bf16[32,128,128]{2,1,0:T(8,128)(2,1)S(1)}, bf16[32,128,128]{2,1,0:T(8,128)(2,1)}, u32[]{:S(2)}) copy-start(bf16[32,128,128]{2,1,0:T(8,128)(2,1)} %param.6) | copy-start | bytes 3145732
  87.2 56.3 %all-to-all-start.1 = ((bf16[128,32,256]{2,1,0:T(8,128)(2,1)}), bf16[128,32,256]{2,1,0:T(8,128)(2,1)}, u32[]{:S(2)}, u32[]{:S(2)}) async-start(bf16[128,32,256]{2,1,0:T(8,128)(2,1)} %copy.43), calls=%async_computation.1 | async-start | bytes 4194304 | tf_op jit(solution)/shard_map/all_to_all | solution.py:45
  143.5 9.4 %slice-start = ((s8[8388608]{0:T(1024)(128)(4,1)}), s8[4194304]{0:T(1024)(128)(4,1)S(1)}, s32[]{:S(2)}) async-start(s8[8388608]{0:T(1024)(128)(4,1)} %bitcast.54), calls=%async_computation.5 | async-start | bytes 8388608
  145.4 7.4 %slice-start.1 = ((s8[8388608]{0:T(1024)(128)(4,1)}), s8[4194304]{0:T(1024)(128)(4,1)S(1)}, s32[]{:S(2)}) async-start(s8[8388608]{0:T(1024)(128)(4,1)} %bitcast.54), calls=%async_computation.6 | async-start | bytes 8388608
  151.6 0.7 copy-start.7
  151.9 0.9 copy-start.2
  151.9 1.0 copy-start.4
  282.9 9.2 %slice-start.2 = ((s8[8388608]{0:T(1024)(128)(4,1)}), s8[4194304]{0:T(1024)(128)(4,1)S(1)}, s32[]{:S(2)}) async-start(s8[8388608]{0:T(1024)(128)(4,1)} %bitcast.56), calls=%async_computation.7 | async-start | bytes 8388608
  283.1 9.0 %slice-start.3 = ((s8[8388608]{0:T(1024)(128)(4,1)}), s8[4194304]{0:T(1024)(128)(4,1)S(1)}, s32[]{:S(2)}) async-start(s8[8388608]{0:T(1024)(128)(4,1)} %bitcast.56), calls=%async_computation.8 | async-start | bytes 8388608
  289.4 1.0 copy-start.3
  289.4 1.2 copy-start.5
  298.5 7.0 %copy-start.6 = (f32[2,512,256]{1,2,0:T(8,128)S(1)}, f32[2,512,256]{1,2,0:T(8,128)}, u32[]{:S(2)}) copy-start(f32[2,512,256]{1,2,0:T(8,128)} %get-tuple-element.9) | copy-start | bytes 3145732
  298.5 56.1 %all-to-all-start.4 = ((bf16[2,2048,256]{2,0,1:T(2,128)(2,1)}), bf16[2,2048,256]{2,0,1:T(2,128)(2,1)S(1)}, u32[]{:S(2)}, u32[]{:S(2)}) async-start(bf16[2,2048,256]{2,0,1:T(2,128)(2,1)} %copy.57), calls=%async_computation.4 | async-start | bytes 4194304 | tf_op jit(solution)/shard_map/all_to_all | solution.py:58
  358.4 4.5 %copy-start.1 = (bf16[32,128,128]{2,1,0:T(8,128)(2,1)S(1)}, bf16[32,128,128]{2,1,0:T(8,128)(2,1)}, u32[]{:S(2)}) copy-start(bf16[32,128,128]{2,1,0:T(8,128)(2,1)} %param.6) | copy-start | bytes 3145732
where the time goes:
time: 364 us; the launch traced here: 363 us
  blocking collectives  176 us (48%)
  waiting for transfers between devices  95.4 us (26%)
  local copies, waits for them, and re-layouts  40.8 us (11%)
  matrix products  33.6 us (9%)
  starting transfers between devices  14 us (4%)
    all_to_all x2, blocking collectives, apply_operator(): lax.all_to_all(sky_map, 'chan', split_axis=1, concat_axis=0, tiled=True)  119 us
    all_to_all x1, blocking collectives, apply_operator(): lax.all_to_all(channel_mixed.astype(jnp.bfloat16), 'chan', split_axis=0,...  56 us
    all_to_all x1, waiting for transfers between devices, on_device(): lax.all_to_all(final_sky, 'chan', split_axis=1, concat_axis=0, tiled=True)  47.8 us
    all_to_all x1, waiting for transfers between devices, apply_operator(): lax.all_to_all(channel_mixed.astype(jnp.bfloat16), 'chan', split_axis=0,...  47.6 us
    dot_general x3, matrix products, project_back(): jnp.einsum('fkl,fkc->flc', beam_table, stacked, preferred_element_type=jn...  13.5 us
    dot_general x2, matrix products, project_out(): jnp.einsum('fkl,flc->fkc', beam_table, mixed_back, preferred_element_type...  12.4 us
    convert_element_type x2, local copies, waits for them, and re-layouts, apply_operator(): sky_map = project_back(beam_table, field_b).astype(jnp.bfloat16)  12.2 us
    convert_element_type x2, local copies, waits for them, and re-layouts, apply_operator(): channel_mixed.astype(jnp.bfloat16)  9.14 us
  transfers between devices with their start and end apart: 2, of which 2 were waited for; matrix products, arithmetic and copies ran while one was open for 1% of the time, Pallas kernels for 0%

commit v1 on v0

--- a/solution.py
+++ b/solution.py
@@ -4,9 +4,8 @@
 from jax.sharding import PartitionSpec as P
 
 ITERS = 2
-
-
 WEIGHT = 0.2
+CHUNKS = 2
 
 
 def project_back(beam_table, field_b):
@@ -48,21 +47,39 @@
     return project_out(beam_table, mixed_back)
 
 
+def split_columns(x, chunks):
+    half = x.shape[2] // 2
+    width = half // chunks
+    return [
+        jnp.concatenate(
+            [x[:, :, i * width:(i + 1) * width], x[:, :, half + i * width:half + (i + 1) * width]], axis=2
+        )
+        for i in range(chunks)
+    ]
+
+
+def join_columns(parts):
+    width = parts[0].shape[2] // 2
+    return jnp.concatenate([p[:, :, :width] for p in parts] + [p[:, :, width:] for p in parts], axis=2)
+
+
 def on_device(beam_table, covariance, noise_var, start_field, probes):
-    field = start_field
-    column_entries = field.shape[2] // 2
+    column_entries = start_field.shape[2] // 2
+    fields = split_columns(start_field, CHUNKS)
+    rhs = split_columns(probes, CHUNKS)
+    noise = noise_var[:, :, None]
     for repeat in range(ITERS):
-        image = apply_operator(beam_table, covariance, field)
-        field = field + WEIGHT * (probes - image - noise_var[:, :, None] * field)
-    final_sky = project_back(beam_table, field.astype(jnp.bfloat16)).astype(jnp.bfloat16)
-    collected_parts = lax.all_to_all(final_sky, "chan", split_axis=1, concat_axis=0, tiled=True)
-    multipole_band_power = (
-        jnp.einsum(
-            "mjk,ujk->jmu", collected_parts, collected_parts, preferred_element_type=jnp.float32
-        )
-        / column_entries
-    )
-    return (field, multipole_band_power.astype(jnp.bfloat16))
+        for i in range(CHUNKS):
+            image = apply_operator(beam_table, covariance, fields[i])
+            fields[i] = fields[i] + WEIGHT * (rhs[i] - image - noise * fields[i])
+    power = None
+    for i in range(CHUNKS):
+        final_sky = project_back(beam_table, fields[i].astype(jnp.bfloat16)).astype(jnp.bfloat16)
+        collected = lax.all_to_all(final_sky, "chan", split_axis=1, concat_axis=0, tiled=True)
+        part = jnp.einsum("mjk,ujk->jmu", collected, collected, preferred_element_type=jnp.float32)
+        power = part if power is None else power + part
+    multipole_band_power = power / column_entries
+    return (join_columns(fields), multipole_band_power.astype(jnp.bfloat16))
 
 
 def solution(mesh):

time: 364 us -> 383 us (1.052)
  blocking collectives: 176 us -> 74.2 us
  waiting for transfers between devices: 95.4 us -> 140 us
  starting transfers between devices: 14 us -> 55.7 us
  matrix products: 33.6 us -> 53.5 us
  local copies, waits for them, and re-layouts: 40.8 us -> 48.4 us
    all_to_all x1 -> x0, blocking collectives: 56 us -> none  [apply_operator(): lax.all_to_all(channel_mixed.astype(jnp.bfloat16), 'chan', split_axis=0,...]
    all_to_all x2, blocking collectives: 119 us -> 74.2 us  [apply_operator(): lax.all_to_all(sky_map, 'chan', split_axis=1, concat_axis=0, tiled=True)]
    all_to_all x0 -> x2, waiting for transfers between devices: none -> 31.6 us  [apply_operator(): lax.all_to_all(sky_map, 'chan', split_axis=1, concat_axis=0, tiled=True)]
    all_to_all x1 -> x4, waiting for transfers between devices: 47.6 us -> 75 us  [apply_operator(): lax.all_to_all(channel_mixed.astype(jnp.bfloat16), 'chan', split_axis=0,...]
    all_to_all x1 -> x4, starting transfers between devices: 7.06 us -> 27.8 us  [apply_operator(): lax.all_to_all(channel_mixed.astype(jnp.bfloat16), 'chan', split_axis=0,...]
    all_to_all x1 -> x2, waiting for transfers between devices: 47.8 us -> 33 us  [on_device(): lax.all_to_all(final_sky, 'chan', split_axis=1, concat_axis=0, tiled=True)]
    all_to_all x0 -> x2, starting transfers between devices: none -> 14 us  [apply_operator(): lax.all_to_all(sky_map, 'chan', split_axis=1, concat_axis=0, tiled=True)]
    dot_general x2 -> x4, matrix products: 12.4 us -> 25.6 us  [project_out(): jnp.einsum('fkl,flc->fkc', beam_table, mixed_back, preferred_element_type...]
  transfers between devices with their start and end apart: 2 -> 8, of which waited for: 2 -> 8; matrix products, arithmetic and copies ran while one was open for 1% -> 19% of each run, Pallas kernels for 0% -> 0%
where the time goes in v1:
time: 383 us; the launch traced here: 378 us
  waiting for transfers between devices  140 us (37%)
  blocking collectives  74.2 us (19%)
  starting transfers between devices  55.7 us (15%)
  matrix products  53.5 us (14%)
  local copies, waits for them, and re-layouts  48.4 us (13%)
  other arithmetic  4.93 us (1%)
    all_to_all x4, waiting for transfers between devices, apply_operator(): lax.all_to_all(channel_mixed.astype(jnp.bfloat16), 'chan', split_axis=0,...  75 us
    all_to_all x2, blocking collectives, apply_operator(): lax.all_to_all(sky_map, 'chan', split_axis=1, concat_axis=0, tiled=True)  74.2 us
    all_to_all x2, waiting for transfers between devices, on_device(): lax.all_to_all(final_sky, 'chan', split_axis=1, concat_axis=0, tiled=True)  33 us
    all_to_all x2, waiting for transfers between devices, apply_operator(): lax.all_to_all(sky_map, 'chan', split_axis=1, concat_axis=0, tiled=True)  31.6 us
    all_to_all x4, starting transfers between devices, apply_operator(): lax.all_to_all(channel_mixed.astype(jnp.bfloat16), 'chan', split_axis=0,...  27.8 us
    dot_general x4, matrix products, project_out(): jnp.einsum('fkl,flc->fkc', beam_table, mixed_back, preferred_element_type...  25.6 us
    dot_general x6, matrix products, project_back(): jnp.einsum('fkl,fkc->flc', beam_table, stacked, preferred_element_type=jn...  21.7 us
    all_to_all x2, starting transfers between devices, apply_operator(): lax.all_to_all(sky_map, 'chan', split_axis=1, concat_axis=0, tiled=True)  14 us
  transfers between devices with their start and end apart: 8, of which 8 were waited for; matrix products, arithmetic and copies ran while one was open for 19% of the time, Pallas kernels for 0%

profile of v1, /device:TPU:2, one launch (start us, length us, event | category | flops | bytes accessed | tf_op | source)
XLA Modules:
  0.0 378.2 jit_solution(6249983274507335066)
XLA Ops:
  0.6 2.7 fusion.71
  4.4 5.6 %fusion = bf16[2,2048,128]{1,2,0:T(8,128)(2,1)} fusion(bf16[2,1024,2048]{2,1,0:T(8,128)(2,1)} %param.5, bf16[2,512,64]{1,2,0:T(8,128)(2,1)S(1)} %get-tuple-element.39, bf16[2,512,64]{1,2,0:T(8,128)(2,1)S(1)} %get-tuple-element.38, bf16[2,512,128]{1,2,0:T(8,128)(2,1)S(1)} %fusion.57), kind=kOutput, calls=%fused_computation.6 | convolution fusion | flops 1075838976 | bytes 9961472 | tf_op jit(solution)/shard_map/fkl,fkc->flc/dot_general | solution.py:17
  10.1 2.4 copy.67
  12.5 40.7 %all_to_all.180 = bf16[2,2048,128]{2,0,1:T(2,128)(2,1)S(1)} all-to-all(bf16[2,2048,128]{2,0,1:T(2,128)(2,1)S(1)} %copy.67), channel_id=1, replica_groups=mesh['chan'=64,'ma'=4] {'chan'}, dimensions={1} | all-to-all | bytes 2097152 | tf_op jit(solution)/shard_map/all_to_all | solution.py:41
  54.4 1.7 copy.71
  56.1 6.9 %all-to-all-start.1 = ((bf16[128,32,128]{2,1,0:T(8,128)(2,1)}), bf16[128,32,128]{2,1,0:T(8,128)(2,1)S(1)}, u32[]{:S(2)}, u32[]{:S(2)}) async-start(bf16[128,32,128]{2,1,0:T(8,128)(2,1)} %copy.71), calls=%async_computation.1 | async-start | bytes 2097152 | tf_op jit(solution)/shard_map/all_to_all | solution.py:44
  65.1 5.7 %fusion.2 = bf16[2,2048,128]{1,2,0:T(8,128)(2,1)} fusion(bf16[2,1024,2048]{2,1,0:T(8,128)(2,1)} %param.5, bf16[2,512,64]{1,2,0:T(8,128)(2,1)S(1)} %get-tuple-element.43, bf16[2,512,64]{1,2,0:T(8,128)(2,1)S(1)} %get-tuple-element.42, bf16[2,512,128]{1,2,0:T(8,128)(2,1)S(1)} %fusion.56), kind=kOutput, calls=%fused_computation.8 | convolution fusion | flops 1075838976 | bytes 9961472 | tf_op jit(solution)/shard_map/fkl,fkc->flc/dot_general | solution.py:17
  70.8 3.7 copy.85
  74.5 15.4 %all-to-all-done.1 = bf16[128,32,128]{2,1,0:T(8,128)(2,1)S(1)} async-done(((bf16[128,32,128]{2,1,0:T(8,128)(2,1)}), bf16[128,32,128]{2,1,0:T(8,128)(2,1)S(1)}, u32[]{:S(2)}, u32[]{:S(2)}) %all-to-all-start.1) | async-done | bytes 1048608 | tf_op jit(solution)/shard_map/all_to_all | solution.py:44
  90.9 7.1 %all-to-all-start.4 = ((bf16[2,2048,128]{2,0,1:T(2,128)(2,1)}), bf16[2,2048,128]{2,0,1:T(2,128)(2,1)S(1)}, u32[]{:S(2)}, u32[]{:S(2)}) async-start(bf16[2,2048,128]{2,0,1:T(2,128)(2,1)} %copy.85), calls=%async_computation.4 | async-start | bytes 2097152 | tf_op jit(solution)/shard_map/all_to_all | solution.py:41
  98.1 1.6 fusion.70
  99.7 1.3 copy.112
  101.0 1.3 copy.113
  102.3 1.5 copy.72
  103.8 6.5 %convolution_bitcast_fusion.3 = f32[2,1024,128]{1,2,0:T(8,128)S(1)} fusion(bf16[2,2048,128]{2,1,0:T(8,128)(2,1)S(1)} %bitcast.99, bf16[2,1024,2048]{2,1,0:T(8,128)(2,1)} %param.5), kind=kOutput, calls=%fused_computation.24 | convolution fusion | flops 1073741824 | bytes 10485760 | tf_op jit(solution)/shard_map/fkl,flc->fkc/dot_general | solution.py:23
  111.1 2.2 fusion.1
  113.3 3.7 copy.74
  117.0 7.6 %all-to-all-done.4 = bf16[2,2048,128]{2,0,1:T(2,128)(2,1)S(1)} async-done(((bf16[2,2048,128]{2,0,1:T(2,128)(2,1)}), bf16[2,2048,128]{2,0,1:T(2,128)(2,1)S(1)}, u32[]{:S(2)}, u32[]{:S(2)}) %all-to-all-start.4) | async-done | bytes 1048608 | tf_op jit(solution)/shard_map/all_to_all | solution.py:41
  124.6 6.9 %all-to-all-start.2 = ((bf16[2,2048,128]{2,0,1:T(2,128)(2,1)}), bf16[2,2048,128]{2,0,1:T(2,128)(2,1)S(1)}, u32[]{:S(2)}, u32[]{:S(2)}) async-start(bf16[2,2048,128]{2,0,1:T(2,128)(2,1)} %copy.74), calls=%async_computation.2 | async-start | bytes 2097152 | tf_op jit(solution)/shard_map/all_to_all | solution.py:41
  132.7 1.7 copy.89
  134.4 23.9 %all-to-all-done.2 = bf16[2,2048,128]{2,0,1:T(2,128)(2,1)S(1)} async-done(((bf16[2,2048,128]{2,0,1:T(2,128)(2,1)}), bf16[2,2048,128]{2,0,1:T(2,128)(2,1)S(1)}, u32[]{:S(2)}, u32[]{:S(2)}) %all-to-all-start.2) | async-done | bytes 1048608 | tf_op jit(solution)/shard_map/all_to_all | solution.py:41
  158.3 6.9 %all-to-all-start.5 = ((bf16[128,32,128]{2,1,0:T(8,128)(2,1)}), bf16[128,32,128]{2,1,0:T(8,128)(2,1)S(1)}, u32[]{:S(2)}, u32[]{:S(2)}) async-start(bf16[128,32,128]{2,1,0:T(8,128)(2,1)} %copy.89), calls=%async_computation.5 | async-start | bytes 2097152 | tf_op jit(solution)/shard_map/all_to_all | solution.py:44
  166.4 1.7 copy.78
  168.0 23.9 %all-to-all-done.5 = bf16[128,32,128]{2,1,0:T(8,128)(2,1)S(1)} async-done(((bf16[128,32,128]{2,1,0:T(8,128)(2,1)}), bf16[128,32,128]{2,1,0:T(8,128)(2,1)S(1)}, u32[]{:S(2)}, u32[]{:S(2)}) %all-to-all-start.5) | async-done | bytes 1048608 | tf_op jit(solution)/shard_map/all_to_all | solution.py:44
  192.0 7.2 %all-to-all-start.3 = ((bf16[128,32,128]{2,1,0:T(8,128)(2,1)}), bf16[128,32,128]{2,1,0:T(8,128)(2,1)S(1)}, u32[]{:S(2)}, u32[]{:S(2)}) async-start(bf16[128,32,128]{2,1,0:T(8,128)(2,1)} %copy.78), calls=%async_computation.3 | async-start | bytes 2097152 | tf_op jit(solution)/shard_map/all_to_all | solution.py:44
  199.2 1.9 copy.116
  201.1 1.9 copy.117
  203.1 6.3 %convolution_bitcast_fusion.1 = f32[2,1024,128]{1,2,0:T(8,128)S(1)} fusion(bf16[2,2048,128]{2,1,0:T(8,128)(2,1)S(1)} %bitcast.102, bf16[2,1024,2048]{2,1,0:T(8,128)(2,1)} %param.5), kind=kOutput, calls=%fused_computation.22 | convolution fusion | flops 1073741824 | bytes 10485760 | tf_op jit(solution)/shard_map/fkl,flc->fkc/dot_general | solution.py:23
  210.3 15.5 %all-to-all-done.3 = bf16[128,32,128]{2,1,0:T(8,128)(2,1)S(1)} async-done(((bf16[128,32,128]{2,1,0:T(8,128)(2,1)}), bf16[128,32,128]{2,1,0:T(8,128)(2,1)S(1)}, u32[]{:S(2)}, u32[]{:S(2)}) %all-to-all-start.3) | async-done | bytes 1048608 | tf_op jit(solution)/shard_map/all_to_all | solution.py:44
  226.0 6.4 %convolution_bitcast_fusion.2 = f32[2,1024,128]{1,2,0:T(8,128)S(1)} fusion(bf16[2,2048,128]{2,1,0:T(8,128)(2,1)S(1)} %bitcast.103, bf16[2,1024,2048]{2,1,0:T(8,128)(2,1)} %param.5), kind=kOutput, calls=%fused_computation.23 | convolution fusion | flops 1073741824 | bytes 10485760 | tf_op jit(solution)/shard_map/fkl,flc->fkc/dot_general | solution.py:23
  232.6 1.3 fusion.68
  234.0 1.3 fusion.3
  236.1 33.5 %all_to_all.181 = bf16[2,2048,128]{2,0,1:T(2,128)(2,1)S(1)} all-to-all(bf16[2,2048,128]{2,0,1:T(2,128)(2,1)S(1)} %copy.92), channel_id=1, replica_groups=mesh['chan'=64,'ma'=4] {'chan'}, dimensions={1} | all-to-all | bytes 2097152 | tf_op jit(solution)/shard_map/all_to_all | solution.py:41
  270.7 1.7 copy.96
  272.4 6.9 %all-to-all-start.7 = ((bf16[128,32,128]{2,1,0:T(8,128)(2,1)}), bf16[128,32,128]{2,1,0:T(8,128)(2,1)S(1)}, u32[]{:S(2)}, u32[]{:S(2)}) async-start(bf16[128,32,128]{2,1,0:T(8,128)(2,1)} %copy.96), calls=%async_computation.7 | async-start | bytes 2097152 | tf_op jit(solution)/shard_map/all_to_all | solution.py:44
  279.3 4.6 %fusion.4 = bf16[2,2048,128]{1,2,0:T(8,128)(2,1)S(1)} fusion(bf16[2,1024,2048]{2,1,0:T(8,128)(2,1)} %param.5, bf16[2,512,64]{1,2,0:T(8,128)(2,1)S(1)} %get-tuple-element.35, bf16[2,512,64]{1,2,0:T(8,128)(2,1)S(1)} %get-tuple-element.34, bf16[2,512,128]{1,2,0:T(8,128)(2,1)S(1)} %copy-done.29), kind=kOutput, calls=%fused_computation.10 | convolution fusion | flops 1075838976 | bytes 9961472 | tf_op jit(solution)/shard_map/fkl,fkc->flc/dot_general | solution.py:17
  283.9 2.0 copy.99
  285.9 20.1 %all-to-all-done.7 = bf16[128,32,128]{2,1,0:T(8,128)(2,1)S(1)} async-done(((bf16[128,32,128]{2,1,0:T(8,128)(2,1)}), bf16[128,32,128]{2,1,0:T(8,128)(2,1)S(1)}, u32[]{:S(2)}, u32[]{:S(2)}) %all-to-all-start.7) | async-done | bytes 1048608 | tf_op jit(solution)/shard_map/all_to_all | solution.py:44
  306.0 6.9 %all-to-all-start.8 = ((bf16[2,2048,128]{2,0,1:T(2,128)(2,1)}), bf16[2,2048,128]{2,0,1:T(2,128)(2,1)S(1)}, u32[]{:S(2)}, u32[]{:S(2)}) async-start(bf16[2,2048,128]{2,0,1:T(2,128)(2,1)} %copy.99), calls=%async_computation.8 | async-start | bytes 2097152 | tf_op jit(solution)/shard_map/all_to_all | solution.py:78
  313.1 6.4 %convolution_bitcast_fusion = f32[2,1024,128]{1,2,0:T(8,128)S(1)} fusion(bf16[2,2048,128]{2,1,0:T(8,128)(2,1)S(1)} %bitcast.105, bf16[2,1024,2048]{2,1,0:T(8,128)(2,1)} %param.5), kind=kOutput, calls=%fused_computation.21 | convolution fusion | flops 1073741824 | bytes 10485760 | tf_op jit(solution)/shard_map/fkl,flc->fkc/dot_general | solution.py:23
  320.7 2.2 fusion.5
  323.0 3.7 copy.102
  326.6 13.0 %all-to-all-done.8 = bf16[2,2048,128]{2,0,1:T(2,128)(2,1)S(1)} async-done(((bf16[2,2048,128]{2,0,1:T(2,128)(2,1)}), bf16[2,2048,128]{2,0,1:T(2,128)(2,1)S(1)}, u32[]{:S(2)}, u32[]{:S(2)}) %all-to-all-start.8) | async-done | bytes 1048608 | tf_op jit(solution)/shard_map/all_to_all | solution.py:78
  339.7 7.0 %all-to-all-start.9 = ((bf16[2,2048,128]{2,0,1:T(2,128)(2,1)}), bf16[2,2048,128]{2,0,1:T(2,128)(2,1)}, u32[]{:S(2)}, u32[]{:S(2)}) async-start(bf16[2,2048,128]{2,0,1:T(2,128)(2,1)} %copy.102), calls=%async_computation.9 | async-start | bytes 2097152 | tf_op jit(solution)/shard_map/all_to_all | solution.py:78
  351.0 2.5 copy.105
  353.5 19.9 %all-to-all-done.9 = bf16[2,2048,128]{2,0,1:T(2,128)(2,1)} async-done(((bf16[2,2048,128]{2,0,1:T(2,128)(2,1)}), bf16[2,2048,128]{2,0,1:T(2,128)(2,1)}, u32[]{:S(2)}, u32[]{:S(2)}) %all-to-all-start.9) | async-done | bytes 1048608 | tf_op jit(solution)/shard_map/all_to_all | solution.py:78
  373.5 1.4 copy.103
  375.9 1.8 multiply_convert_fusion
  (118 shorter events, 18.1 us)
Async XLA Ops:
  0.6 52.9 %copy-start = (bf16[32,128,128]{2,1,0:T(8,128)(2,1)S(1)}, bf16[32,128,128]{2,1,0:T(8,128)(2,1)}, u32[]{:S(2)}) copy-start(bf16[32,128,128]{2,1,0:T(8,128)(2,1)} %param.6) | copy-start | bytes 3145732
  3.7 0.7 copy-start.3
  56.1 33.8 %all-to-all-start.1 = ((bf16[128,32,128]{2,1,0:T(8,128)(2,1)}), bf16[128,32,128]{2,1,0:T(8,128)(2,1)S(1)}, u32[]{:S(2)}, u32[]{:S(2)}) async-start(bf16[128,32,128]{2,1,0:T(8,128)(2,1)} %copy.71), calls=%async_computation.1 | async-start | bytes 2097152 | tf_op jit(solution)/shard_map/all_to_all | solution.py:44
  64.2 0.7 copy-start.6
  64.4 0.7 copy-start.9
  65.1 33.0 %copy-start.1 = (f32[2,512,256]{2,1,0:T(8,128)S(1)}, f32[2,512,256]{2,1,0:T(8,128)}, u32[]{:S(2)}) copy-start(f32[2,512,256]{2,1,0:T(8,128)} %param.9) | copy-start | bytes 3145732
  89.9 1.0 copy-start.2
  90.9 33.7 %all-to-all-start.4 = ((bf16[2,2048,128]{2,0,1:T(2,128)(2,1)}), bf16[2,2048,128]{2,0,1:T(2,128)(2,1)S(1)}, u32[]{:S(2)}, u32[]{:S(2)}) async-start(bf16[2,2048,128]{2,0,1:T(2,128)(2,1)} %copy.85), calls=%async_computation.4 | async-start | bytes 2097152 | tf_op jit(solution)/shard_map/all_to_all | solution.py:41
  99.7 10.7 %copy-start.4 = (f32[2,512,64]{1,2,0:T(8,128)S(1)}, f32[2,512,64]{1,2,0:T(8,128)}, u32[]{:S(2)}) copy-start(f32[2,512,64]{1,2,0:T(8,128)} %copy-done.3) | copy-start | bytes 786436
  99.7 10.7 %copy-start.30 = (f32[2,512]{1,0:T(2,128)S(1)}, f32[2,512]{1,0:T(2,128)}, u32[]{:S(2)}) copy-start(f32[2,512]{1,0:T(2,128)} %param.7) | copy-start | bytes 12292
  101.0 9.6 %copy-start.12 = (f32[2,512,64]{1,2,0:T(8,128)}, f32[2,512,64]{1,2,0:T(8,128)S(1)}, u32[]{:S(2)}) copy-start(f32[2,512,64]{1,2,0:T(8,128)S(1)} %copy.112) | copy-start | bytes 786436
  102.3 11.0 %copy-start.14 = (f32[2,512,64]{1,2,0:T(8,128)}, f32[2,512,64]{1,2,0:T(8,128)S(1)}, u32[]{:S(2)}) copy-start(f32[2,512,64]{1,2,0:T(8,128)S(1)} %copy.113) | copy-start | bytes 786436
  102.3 8.8 %slice-start = ((s8[8388608]{0:T(1024)(128)(4,1)}), s8[4194304]{0:T(1024)(128)(4,1)S(1)}, s32[]{:S(2)}) async-start(s8[8388608]{0:T(1024)(128)(4,1)} %bitcast.90), calls=%async_computation.10 | async-start | bytes 8388608
  103.8 7.3 %slice-start.1 = ((s8[8388608]{0:T(1024)(128)(4,1)}), s8[4194304]{0:T(1024)(128)(4,1)S(1)}, s32[]{:S(2)}) async-start(s8[8388608]{0:T(1024)(128)(4,1)} %bitcast.90), calls=%async_computation.11 | async-start | bytes 8388608
  110.4 0.7 copy-start.18
  110.4 2.9 copy-start.16
  124.6 33.7 %all-to-all-start.2 = ((bf16[2,2048,128]{2,0,1:T(2,128)(2,1)}), bf16[2,2048,128]{2,0,1:T(2,128)(2,1)S(1)}, u32[]{:S(2)}, u32[]{:S(2)}) async-start(bf16[2,2048,128]{2,0,1:T(2,128)(2,1)} %copy.74), calls=%async_computation.2 | async-start | bytes 2097152 | tf_op jit(solution)/shard_map/all_to_all | solution.py:41
  158.3 33.7 %all-to-all-start.5 = ((bf16[128,32,128]{2,1,0:T(8,128)(2,1)}), bf16[128,32,128]{2,1,0:T(8,128)(2,1)S(1)}, u32[]{:S(2)}, u32[]{:S(2)}) async-start(bf16[128,32,128]{2,1,0:T(8,128)(2,1)} %copy.89), calls=%async_computation.5 | async-start | bytes 2097152 | tf_op jit(solution)/shard_map/all_to_all | solution.py:44
  192.0 33.9 %all-to-all-start.3 = ((bf16[128,32,128]{2,1,0:T(8,128)(2,1)}), bf16[128,32,128]{2,1,0:T(8,128)(2,1)S(1)}, u32[]{:S(2)}, u32[]{:S(2)}) async-start(bf16[128,32,128]{2,1,0:T(8,128)(2,1)} %copy.78), calls=%async_computation.3 | async-start | bytes 2097152 | tf_op jit(solution)/shard_map/all_to_all | solution.py:44
  209.4 23.1 %copy-start.5 = (f32[2,512,64]{1,2,0:T(8,128)S(1)}, f32[2,512,64]{1,2,0:T(8,128)}, u32[]{:S(2)}) copy-start(f32[2,512,64]{1,2,0:T(8,128)} %copy-done.3) | copy-start | bytes 786436
  209.4 23.1 %copy-start.7 = (f32[2,512,64]{1,2,0:T(8,128)S(1)}, f32[2,512,64]{1,2,0:T(8,128)}, u32[]{:S(2)}) copy-start(f32[2,512,64]{1,2,0:T(8,128)} %copy-done.6) | copy-start | bytes 786436
  209.4 23.1 %copy-start.10 = (f32[2,512,64]{1,2,0:T(8,128)S(1)}, f32[2,512,64]{1,2,0:T(8,128)}, u32[]{:S(2)}) copy-start(f32[2,512,64]{1,2,0:T(8,128)} %copy-done.9) | copy-start | bytes 786436
  209.4 23.1 %copy-start.13 = (f32[2,512,64]{1,2,0:T(8,128)S(1)}, f32[2,512,64]{1,2,0:T(8,128)}, u32[]{:S(2)}) copy-start(f32[2,512,64]{1,2,0:T(8,128)} %copy-done.12) | copy-start | bytes 786436
  225.8 6.7 %copy-start.15 = (f32[2,512,64]{1,2,0:T(8,128)S(1)}, f32[2,512,64]{1,2,0:T(8,128)}, u32[]{:S(2)}) copy-start(f32[2,512,64]{1,2,0:T(8,128)} %copy-done.14) | copy-start | bytes 786436
  225.8 6.7 %copy-start.17 = (f32[2,512,64]{1,2,0:T(8,128)S(1)}, f32[2,512,64]{1,2,0:T(8,128)}, u32[]{:S(2)}) copy-start(f32[2,512,64]{1,2,0:T(8,128)} %copy-done.16) | copy-start | bytes 786436
  225.8 6.7 %copy-start.19 = (f32[2,512,64]{1,2,0:T(8,128)S(1)}, f32[2,512,64]{1,2,0:T(8,128)}, u32[]{:S(2)}) copy-start(f32[2,512,64]{1,2,0:T(8,128)} %copy-done.18) | copy-start | bytes 786436
  225.8 6.7 %copy-start.20 = (f32[2,512,64]{1,2,0:T(8,128)S(1)}, f32[2,512,64]{1,2,0:T(8,128)}, u32[]{:S(2)}) copy-start(f32[2,512,64]{1,2,0:T(8,128)} %copy.116) | copy-start | bytes 786436
  225.8 6.7 %copy-start.22 = (f32[2,512,64]{1,2,0:T(8,128)S(1)}, f32[2,512,64]{1,2,0:T(8,128)}, u32[]{:S(2)}) copy-start(f32[2,512,64]{1,2,0:T(8,128)} %copy.117) | copy-start | bytes 786436
  225.8 6.7 %copy-start.24 = (f32[2,512,64]{1,2,0:T(8,128)S(1)}, f32[2,512,64]{1,2,0:T(8,128)}, u32[]{:S(2)}) copy-start(f32[2,512,64]{1,2,0:T(8,128)} %get-tuple-element.26) | copy-start | bytes 786436
  225.8 6.7 %copy-start.26 = (f32[2,512,64]{1,2,0:T(8,128)S(1)}, f32[2,512,64]{1,2,0:T(8,128)}, u32[]{:S(2)}) copy-start(f32[2,512,64]{1,2,0:T(8,128)} %get-tuple-element.27) | copy-start | bytes 786436
  225.9 8.1 %slice-start.2 = ((s8[8388608]{0:T(1024)(128)(4,1)}), s8[4194304]{0:T(1024)(128)(4,1)S(1)}, s32[]{:S(2)}) async-start(s8[8388608]{0:T(1024)(128)(4,1)} %bitcast.92), calls=%async_computation.12 | async-start | bytes 8388608
  226.0 8.0 %slice-start.3 = ((s8[8388608]{0:T(1024)(128)(4,1)}), s8[4194304]{0:T(1024)(128)(4,1)S(1)}, s32[]{:S(2)}) async-start(s8[8388608]{0:T(1024)(128)(4,1)} %bitcast.92), calls=%async_computation.13 | async-start | bytes 8388608
  235.3 44.0 %copy-start.29 = (bf16[2,512,128]{1,2,0:T(8,128)(2,1)S(1)}, bf16[2,512,128]{1,2,0:T(8,128)(2,1)}, u32[]{:S(2)}) copy-start(bf16[2,512,128]{1,2,0:T(8,128)(2,1)} %get-tuple-element.10) | copy-start | bytes 786436
  272.4 33.7 %all-to-all-start.7 = ((bf16[128,32,128]{2,1,0:T(8,128)(2,1)}), bf16[128,32,128]{2,1,0:T(8,128)(2,1)S(1)}, u32[]{:S(2)}, u32[]{:S(2)}) async-start(bf16[128,32,128]{2,1,0:T(8,128)(2,1)} %copy.96), calls=%async_computation.7 | async-start | bytes 2097152 | tf_op jit(solution)/shard_map/all_to_all | solution.py:44
  285.9 33.6 %copy-start.8 = (f32[2,512,64]{1,2,0:T(8,128)S(1)}, f32[2,512,64]{1,2,0:T(8,128)}, u32[]{:S(2)}) copy-start(f32[2,512,64]{1,2,0:T(8,128)} %copy-done.6) | copy-start | bytes 786436
  306.0 33.7 %all-to-all-start.8 = ((bf16[2,2048,128]{2,0,1:T(2,128)(2,1)}), bf16[2,2048,128]{2,0,1:T(2,128)(2,1)S(1)}, u32[]{:S(2)}, u32[]{:S(2)}) async-start(bf16[2,2048,128]{2,0,1:T(2,128)(2,1)} %copy.99), calls=%async_computation.8 | async-start | bytes 2097152 | tf_op jit(solution)/shard_map/all_to_all | solution.py:78
  312.9 6.7 %copy-start.11 = (f32[2,512,64]{1,2,0:T(8,128)S(1)}, f32[2,512,64]{1,2,0:T(8,128)}, u32[]{:S(2)}) copy-start(f32[2,512,64]{1,2,0:T(8,128)} %copy-done.9) | copy-start | bytes 786436
  312.9 6.7 %copy-start.21 = (f32[2,512,64]{1,2,0:T(8,128)S(1)}, f32[2,512,64]{1,2,0:T(8,128)}, u32[]{:S(2)}) copy-start(f32[2,512,64]{1,2,0:T(8,128)} %copy.116) | copy-start | bytes 786436
  312.9 6.7 %copy-start.23 = (f32[2,512,64]{1,2,0:T(8,128)S(1)}, f32[2,512,64]{1,2,0:T(8,128)}, u32[]{:S(2)}) copy-start(f32[2,512,64]{1,2,0:T(8,128)} %copy.117) | copy-start | bytes 786436
  312.9 6.7 %copy-start.25 = (f32[2,512,64]{1,2,0:T(8,128)S(1)}, f32[2,512,64]{1,2,0:T(8,128)}, u32[]{:S(2)}) copy-start(f32[2,512,64]{1,2,0:T(8,128)} %get-tuple-element.26) | copy-start | bytes 786436
  312.9 6.7 %copy-start.27 = (f32[2,512,64]{1,2,0:T(8,128)S(1)}, f32[2,512,64]{1,2,0:T(8,128)}, u32[]{:S(2)}) copy-start(f32[2,512,64]{1,2,0:T(8,128)} %get-tuple-element.27) | copy-start | bytes 786436
  313.0 7.8 %slice-start.4 = ((s8[8388608]{0:T(1024)(128)(4,1)}), s8[4194304]{0:T(1024)(128)(4,1)S(1)}, s32[]{:S(2)}) async-start(s8[8388608]{0:T(1024)(128)(4,1)} %bitcast.94), calls=%async_computation.14 | async-start | bytes 8388608
  313.0 7.7 %slice-start.5 = ((s8[8388608]{0:T(1024)(128)(4,1)}), s8[4194304]{0:T(1024)(128)(4,1)S(1)}, s32[]{:S(2)}) async-start(s8[8388608]{0:T(1024)(128)(4,1)} %bitcast.94), calls=%async_computation.15 | async-start | bytes 8388608
  320.7 26.0 %copy-start.28 = (f32[2,512,128]{1,2,0:T(8,128)S(1)}, f32[2,512,128]{1,2,0:T(8,128)}, u32[]{:S(2)}) copy-start(f32[2,512,128]{1,2,0:T(8,128)} %get-tuple-element.11) | copy-start | bytes 1572868
  339.7 33.8 %all-to-all-start.9 = ((bf16[2,2048,128]{2,0,1:T(2,128)(2,1)}), bf16[2,2048,128]{2,0,1:T(2,128)(2,1)}, u32[]{:S(2)}, u32[]{:S(2)}) async-start(bf16[2,2048,128]{2,0,1:T(2,128)(2,1)} %copy.102), calls=%async_computation.9 | async-start | bytes 2097152 | tf_op jit(solution)/shard_map/all_to_all | solution.py:78

commit v2 on v0

v2 whole, which is shorter than its diff:
```python
import functools

import jax
import jax.numpy as jnp
from jax import lax
from jax.experimental import pallas as pl
from jax.experimental.pallas import tpu as pltpu
from jax.sharding import PartitionSpec as P

ITERS = 2
WEIGHT = 0.2
L_BLOCK = 512


def stack_transposed(field):
    field_b = field.astype(jnp.bfloat16)
    half = field_b.shape[2] // 2
    reals = field_b[:, :, :half]
    imags = field_b[:, :, half:]
    lower = jnp.concatenate([imags, -reals], axis=2)
    stacked = jnp.concatenate([field_b, lower], axis=1)
    return jnp.swapaxes(stacked, 1, 2)


def _back_kernel(st_ref, b_ref, out_ref):
    acc = jnp.dot(st_ref[0], b_ref[0], preferred_element_type=jnp.float32)
    out_ref[...] = acc.T.astype(out_ref.dtype)


def project_back(beam_table, field):
    channels, rows, multipoles = beam_table.shape
    stacked_t = stack_transposed(field)
    columns = stacked_t.shape[1]
    blocks = multipoles // L_BLOCK
    return pl.pallas_call(
        _back_kernel,
        grid=(channels, blocks),
        in_specs=[
            pl.BlockSpec((1, columns, rows), lambda f, i: (f, 0, 0)),
            pl.BlockSpec((1, rows, L_BLOCK), lambda f, i: (f, 0, i)),
        ],
        out_specs=pl.BlockSpec((L_BLOCK, columns), lambda f, i: (i, f)),
        out_shape=jax.ShapeDtypeStruct((multipoles, channels * columns), jnp.bfloat16),
        cost_estimate=pl.CostEstimate(
            flops=2 * channels * rows * multipoles * columns,
            transcendentals=0,
            bytes_accessed=2 * (channels * rows * multipoles + channels * columns * rows + multipoles * channels * columns),
        ),
    )(stacked_t, beam_table)


def gather_sky(sky, devices):
    received = lax.all_to_all(sky, "chan", split_axis=0, concat_axis=0, tiled=True)
    local = received.shape[0] // devices
    split = received.reshape(devices, local, 2, received.shape[1] // 2)
    return jnp.transpose(split, (1, 0, 2, 3)).reshape(local, 2 * devices, received.shape[1] // 2)


def project_out(beam_table, mixed_back):
    column_entries = mixed_back.shape[2] // 2
    modes = beam_table.shape[1] // 2
    product = jnp.einsum("fkl,flc->fkc", beam_table, mixed_back, preferred_element_type=jnp.float32)
    upper = product[:, :modes]
    lower = product[:, modes:]
    return jnp.concatenate(
        [
            upper[:, :, :column_entries] - lower[:, :, column_entries:],
            upper[:, :, column_entries:] + lower[:, :, :column_entries],
        ],
        axis=2,
    )


def apply_operator(beam_table, covariance, field, devices):
    sky = gather_sky(project_back(beam_table, field), devices)
    channel_mixed = jnp.einsum("jpg,jgc->pjc", covariance, sky, preferred_element_type=jnp.float32)
    mixed_back = lax.all_to_all(
        channel_mixed.astype(jnp.bfloat16), "chan", split_axis=0, concat_axis=1, tiled=True
    )
    return project_out(beam_table, mixed_back)


def on_device(beam_table, covariance, noise_var, start_field, probes):
    devices = lax.axis_size("chan")
    column_entries = start_field.shape[2] // 2
    local, channels, _ = covariance.shape
    field = start_field
    for repeat in range(ITERS):
        image = apply_operator(beam_table, covariance, field, devices)
        field = field + WEIGHT * (probes - image - noise_var[:, :, None] * field)
    final_sky = gather_sky(project_back(beam_table, field), devices)
    power = jnp.einsum("jpc,jqc->jpq", final_sky, final_sky, preferred_element_type=jnp.float32) / column_entries
    return (field, power.astype(jnp.bfloat16))


def solution(mesh):
    return jax.shard_map(
        on_device,
        mesh=mesh,
        in_specs=(
            P(("ma", "chan"), None, None),
            P(("ma", "chan"), None, None),
            P(("ma", "chan"), None),
            P(("ma", "chan"), None, None),
            P(("ma", "chan"), None, None),
        ),
        out_specs=(P(("ma", "chan"), None, None), P(("ma", "chan"), None, None)),
        check_vma=False,
    )
```

time: 364 us -> 380 us (1.044)
  Pallas kernels: 0 us -> 27.1 us
  matrix products: 33.6 us -> 19.9 us
    pallas_call x0 -> x3, Pallas kernels: none -> 27.1 us  [project_back(): pl.pallas_call(_back_kernel, grid=(channels, blocks), in_specs=[pl.BlockS...]
    reshape x0 -> x5, local copies, waits for them, and re-layouts: none -> 18 us  [the longest x4 15.1 us: gather_sky(): split = received.reshape(devices, local, 2, received.shape[1] // 2)]
    convert_element_type x3 -> x0, local copies, waits for them, and re-layouts: 16.1 us -> none  [the longest x2 12.2 us: apply_operator(): sky_map = project_back(beam_table, field_b).astype(jnp.bfloat16)]
    dot_general x6 -> x3, matrix products: 21.2 us -> 7.73 us  [the longest x2 6.04 us: apply_operator(): jnp.einsum('jpg,jgc->pjc', covariance, sky, preferred_element_type=jnp.fl...]
    all_to_all x7 -> x0, local copies, waits for them, and re-layouts: 7.49 us -> none  [the longest x3 6.6 us: on_device(): lax.all_to_all(final_sky, 'chan', split_axis=1, concat_axis=0, tiled=True)]
    transpose x0 -> x2, local copies, waits for them, and re-layouts: none -> 4.12 us  [gather_sky(): jnp.transpose(split, (1, 0, 2, 3))]
where the time goes in v2:
time: 380 us; the launch traced here: 378 us
  blocking collectives  176 us (46%)
  waiting for transfers between devices  95.4 us (25%)
  local copies, waits for them, and re-layouts  39.2 us (10%)
  Pallas kernels  27.1 us (7%)
  matrix products  19.9 us (5%)
  starting transfers between devices  14 us (4%)
  other arithmetic  5.81 us (2%)
    all_to_all x2, blocking collectives, gather_sky(): lax.all_to_all(sky, 'chan', split_axis=0, concat_axis=0, tiled=True)  120 us
    all_to_all x1, blocking collectives, apply_operator(): lax.all_to_all(channel_mixed.astype(jnp.bfloat16), 'chan', split_axis=0,...  56 us
    all_to_all x1, waiting for transfers between devices, gather_sky(): lax.all_to_all(sky, 'chan', split_axis=0, concat_axis=0, tiled=True)  47.8 us
    all_to_all x1, waiting for transfers between devices, apply_operator(): lax.all_to_all(channel_mixed.astype(jnp.bfloat16), 'chan', split_axis=0,...  47.6 us
    pallas_call x3, Pallas kernels, project_back(): pl.pallas_call(_back_kernel, grid=(channels, blocks), in_specs=[pl.BlockS...  27.1 us
    reshape x4, local copies, waits for them, and re-layouts, gather_sky(): split = received.reshape(devices, local, 2, received.shape[1] // 2)  15.1 us
    dot_general x2, matrix products, project_out(): jnp.einsum('fkl,flc->fkc', beam_table, mixed_back, preferred_element_type...  12.1 us
    convert_element_type x2, local copies, waits for them, and re-layouts, apply_operator(): channel_mixed.astype(jnp.bfloat16)  9.17 us
  transfers between devices with their start and end apart: 2, of which 2 were waited for; matrix products, arithmetic and copies ran while one was open for 1% of the time, Pallas kernels for 0%

profile of v2, /device:TPU:2, one launch (start us, length us, event | category | flops | bytes accessed | tf_op | source)
XLA Modules:
  0.0 378.0 jit_solution(6750430960721799057)
XLA Ops:
  0.6 0.0 copy-start
  0.6 1.6 copy.58
  2.3 0.1 convert_element_type.24
  2.4 1.1 maximum_bitcast_fusion.st_ref
  3.5 9.0 %shard_map.68 = bf16[2048,512]{1,0:T(8,128)(2,1)} custom-call(bf16[2,256,1024]{2,1,0:T(8,128)(2,1)} %maximum_bitcast_fusion.st_ref, bf16[2,1024,2048]{2,1,0:T(8,128)(2,1)} %b_ref.5), custom_call_target="tpu_custom_call" | custom-call | flops 2147483648 | bytes 11534336 | tf_op jit(solution)/shard_map/pallas_call | solution.py:35
  12.6 63.5 %all_to_all.63 = bf16[64,32,512]{2,1,0:T(8,128)(2,1)} all-to-all(bf16[64,32,512]{2,1,0:T(8,128)(2,1)} %bitcast.47), channel_id=1, replica_groups=mesh['chan'=64,'ma'=4] {'chan'}, dimensions={0} | all-to-all | bytes 4194304 | tf_op jit(solution)/shard_map/all_to_all | solution.py:53
  76.1 4.0 %reshape.32 = bf16[64,32,2,256]{3,2,1,0:T(2,128)(2,1)} reshape(bf16[64,32,512]{2,1,0:T(8,128)(2,1)} %all_to_all.63) | data formatting | bytes 4194304 | tf_op jit(solution)/shard_map/reshape | solution.py:55
  80.1 2.1 copy.51
  82.1 0.0 copy-done
  82.1 3.0 convert_bitcast_fusion.1
  85.1 4.6 %copy.53 = bf16[128,32,256]{2,1,0:T(8,128)(2,1)} copy(bf16[128,32,256]{0,2,1:T(8,128)(2,1)} %convert_bitcast_fusion.1) | data formatting | bytes 4194304 | tf_op jit(solution)/shard_map/convert_element_type | solution.py:78
  89.8 7.0 %all-to-all-start.1 = ((bf16[128,32,256]{2,1,0:T(8,128)(2,1)}), bf16[128,32,256]{2,1,0:T(8,128)(2,1)}, u32[]{:S(2)}, u32[]{:S(2)}) async-start(bf16[128,32,256]{2,1,0:T(8,128)(2,1)} %copy.53), calls=%async_computation.1 | async-start | bytes 4194304 | tf_op jit(solution)/shard_map/all_to_all | solution.py:77
  96.8 1.6 copy.56
  98.4 47.6 %all-to-all-done.1 = bf16[128,32,256]{2,1,0:T(8,128)(2,1)} async-done(((bf16[128,32,256]{2,1,0:T(8,128)(2,1)}), bf16[128,32,256]{2,1,0:T(8,128)(2,1)}, u32[]{:S(2)}, u32[]{:S(2)}) %all-to-all-start.1) | async-done | bytes 2097184 | tf_op jit(solution)/shard_map/all_to_all | solution.py:77
  146.0 1.8 copy.54
  147.8 6.1 %convolution_bitcast_fusion.1 = f32[2,1024,256]{1,2,0:T(8,128)S(1)} fusion(bf16[2,2048,256]{2,1,0:T(8,128)(2,1)S(1)} %bitcast.49, bf16[2,1024,2048]{2,1,0:T(8,128)(2,1)} %b_ref.5), kind=kOutput, calls=%fused_computation.9 | convolution fusion | flops 2147483648 | bytes 12582912 | tf_op jit(solution)/shard_map/fkl,flc->fkc/dot_general | solution.py:62
  153.9 0.0 copy-start.7
  153.9 0.2 slice_subtract_fusion.1
  154.1 0.0 copy-start.2
  154.1 0.0 copy-start.4
  154.1 0.4 copy-done.7
  154.6 0.4 fusion.14
  155.0 0.0 copy-done.4
  155.1 1.1 maximum_bitcast_fusion.1.st_ref
  156.2 9.0 %shard_map.69 = bf16[2048,512]{1,0:T(8,128)(2,1)} custom-call(bf16[2,256,1024]{2,1,0:T(8,128)(2,1)} %maximum_bitcast_fusion.1.st_ref, bf16[2,1024,2048]{2,1,0:T(8,128)(2,1)} %b_ref.5), custom_call_target="tpu_custom_call" | custom-call | flops 2147483648 | bytes 11534336 | tf_op jit(solution)/shard_map/pallas_call | solution.py:35
  165.2 56.2 %all_to_all.64 = bf16[64,32,512]{2,1,0:T(8,128)(2,1)} all-to-all(bf16[64,32,512]{2,1,0:T(8,128)(2,1)} %bitcast.48), channel_id=1, replica_groups=mesh['chan'=64,'ma'=4] {'chan'}, dimensions={0} | all-to-all | bytes 4194304 | tf_op jit(solution)/shard_map/all_to_all | solution.py:53
  221.4 4.0 %reshape.34 = bf16[64,32,2,256]{3,2,1,0:T(2,128)(2,1)} reshape(bf16[64,32,512]{2,1,0:T(8,128)(2,1)} %all_to_all.64) | data formatting | bytes 4194304 | tf_op jit(solution)/shard_map/reshape | solution.py:55
  225.4 2.1 copy.59
  227.4 3.0 convert_bitcast_fusion
  230.5 4.5 %copy.61 = bf16[128,32,256]{2,1,0:T(8,128)(2,1)} copy(bf16[128,32,256]{0,2,1:T(8,128)(2,1)} %convert_bitcast_fusion) | data formatting | bytes 4194304 | tf_op jit(solution)/shard_map/convert_element_type | solution.py:78
  235.0 56.0 %all_to_all.65 = bf16[128,32,256]{2,1,0:T(8,128)(2,1)S(1)} all-to-all(bf16[128,32,256]{2,1,0:T(8,128)(2,1)} %copy.61), channel_id=1, replica_groups=mesh['chan'=64,'ma'=4] {'chan'}, dimensions={0} | all-to-all | bytes 4194304 | tf_op jit(solution)/shard_map/all_to_all | solution.py:77
  291.0 0.2 copy.62
  291.2 6.1 %convolution_bitcast_fusion = f32[2,1024,256]{1,2,0:T(8,128)S(1)} fusion(bf16[2,2048,256]{2,1,0:T(8,128)(2,1)S(1)} %bitcast.50, bf16[2,1024,2048]{2,1,0:T(8,128)(2,1)} %b_ref.5), kind=kOutput, calls=%fused_computation.8 | convolution fusion | flops 2147483648 | bytes 12582912 | tf_op jit(solution)/shard_map/fkl,flc->fkc/dot_general | solution.py:62
  297.3 0.0 copy-start.5
  297.3 0.2 slice_subtract_fusion
  297.6 0.8 copy-done.3
  298.4 0.2 copy-done.5
  298.5 1.5 fusion.15
  300.1 1.1 maximum_bitcast_fusion.2.st_ref
  301.2 9.0 %shard_map.70 = bf16[2048,512]{1,0:T(8,128)(2,1)} custom-call(bf16[2,256,1024]{2,1,0:T(8,128)(2,1)} %maximum_bitcast_fusion.2.st_ref, bf16[2,1024,2048]{2,1,0:T(8,128)(2,1)} %b_ref.5), custom_call_target="tpu_custom_call" | custom-call | flops 2147483648 | bytes 11534336 | tf_op jit(solution)/shard_map/pallas_call | solution.py:35
  310.2 7.0 %all-to-all-start.4 = ((bf16[64,32,512]{2,1,0:T(8,128)(2,1)}), bf16[64,32,512]{2,1,0:T(8,128)(2,1)S(1)}, u32[]{:S(2)}, u32[]{:S(2)}) async-start(bf16[64,32,512]{2,1,0:T(8,128)(2,1)} %bitcast.46), calls=%async_computation.4 | async-start | bytes 4194304 | tf_op jit(solution)/shard_map/all_to_all | solution.py:53
  317.2 1.3 copy.66
  318.5 47.8 %all-to-all-done.4 = bf16[64,32,512]{2,1,0:T(8,128)(2,1)S(1)} async-done(((bf16[64,32,512]{2,1,0:T(8,128)(2,1)}), bf16[64,32,512]{2,1,0:T(8,128)(2,1)S(1)}, u32[]{:S(2)}, u32[]{:S(2)}) %all-to-all-start.4) | async-done | bytes 2097184 | tf_op jit(solution)/shard_map/all_to_all | solution.py:53
  366.3 2.1 reshape.36
  368.4 5.1 %copy.78 = bf16[64,32,2,256]{3,2,0,1:T(2,128)(2,1)} copy(bf16[64,32,2,256]{3,2,1,0:T(2,128)(2,1)} %reshape.36) | data formatting | bytes 4194304 | tf_op jit(solution)/shard_map/reshape | solution.py:55
  373.5 2.8 reshape.37
  376.3 1.7 multiply_convert_fusion
  378.0 0.0 copy-done.1
  (8 shorter events, 0.1 us)
Async XLA Ops:
  0.6 81.5 %copy-start = (bf16[32,128,128]{2,1,0:T(8,128)(2,1)S(1)}, bf16[32,128,128]{2,1,0:T(8,128)(2,1)}, u32[]{:S(2)}) copy-start(bf16[32,128,128]{2,1,0:T(8,128)(2,1)} %param.6) | copy-start | bytes 3145732
  89.8 56.2 %all-to-all-start.1 = ((bf16[128,32,256]{2,1,0:T(8,128)(2,1)}), bf16[128,32,256]{2,1,0:T(8,128)(2,1)}, u32[]{:S(2)}, u32[]{:S(2)}) async-start(bf16[128,32,256]{2,1,0:T(8,128)(2,1)} %copy.53), calls=%async_computation.1 | async-start | bytes 4194304 | tf_op jit(solution)/shard_map/all_to_all | solution.py:77
  153.9 0.7 copy-start.7
  154.1 0.9 copy-start.2
  154.1 1.0 copy-start.4
  297.3 1.0 copy-start.3
  297.3 1.2 copy-start.5
  310.2 7.0 %copy-start.6 = (f32[2,512,256]{1,2,0:T(8,128)S(1)}, f32[2,512,256]{1,2,0:T(8,128)}, u32[]{:S(2)}) copy-start(f32[2,512,256]{1,2,0:T(8,128)} %get-tuple-element.11) | copy-start | bytes 3145732
  310.2 56.1 %all-to-all-start.4 = ((bf16[64,32,512]{2,1,0:T(8,128)(2,1)}), bf16[64,32,512]{2,1,0:T(8,128)(2,1)S(1)}, u32[]{:S(2)}, u32[]{:S(2)}) async-start(bf16[64,32,512]{2,1,0:T(8,128)(2,1)} %bitcast.46), calls=%async_computation.4 | async-start | bytes 4194304 | tf_op jit(solution)/shard_map/all_to_all | solution.py:53
  373.5 4.5 %copy-start.1 = (bf16[32,128,128]{2,1,0:T(8,128)(2,1)S(1)}, bf16[32,128,128]{2,1,0:T(8,128)(2,1)}, u32[]{:S(2)}) copy-start(bf16[32,128,128]{2,1,0:T(8,128)(2,1)} %param.6) | copy-start | bytes 3145732

commit v3 on v0

v3 whole, which is shorter than its diff:
```python
import functools

import jax
import jax.numpy as jnp
from jax import lax
from jax.experimental import pallas as pl
from jax.experimental.pallas import tpu as pltpu
from jax.sharding import PartitionSpec as P

ITERS = 2
WEIGHT = 0.2
ROW_BLOCK = 256


def _stack_t(new):
    half = new.shape[1] // 2
    t = new.astype(jnp.bfloat16).astype(jnp.float32).T
    zr_t = t[:half]
    zi_t = t[half:]
    top = jnp.concatenate([zr_t, zi_t], axis=1)
    bottom = jnp.concatenate([zi_t, -zr_t], axis=1)
    return jnp.concatenate([top, bottom], axis=0).astype(jnp.bfloat16)


def _sweep_kernel(with_update, *refs):
    if with_update:
        b_hbm, m_hbm, f_hbm, p_hbm, n_hbm, fld_out, sky_out, bv, mv, fv, pv, nv, sems = refs
    else:
        b_hbm, f_hbm, sky_out, bv, fv, sems = refs
    channels, rows, multipoles = bv.shape
    modes = fv.shape[1]
    blocks = modes // ROW_BLOCK
    slot = iter(range(sems.shape[0]))

    def start(src, dst):
        copy = pltpu.make_async_copy(src, dst, sems.at[next(slot)])
        copy.start()
        return copy

    small, beams = [], []
    for f in range(channels):
        group = [start(f_hbm.at[f], fv.at[f])]
        if with_update:
            group += [start(m_hbm.at[:, f], mv.at[f]), start(p_hbm.at[f], pv.at[f]), start(n_hbm.at[f], nv.at[f])]
        small.append(group)
        parts = []
        for kb in range(blocks):
            for base in (0, modes):
                lo = base + kb * ROW_BLOCK
                parts.append(start(b_hbm.at[f, pl.ds(lo, ROW_BLOCK)], bv.at[f, pl.ds(lo, ROW_BLOCK)]))
        beams.append(parts)

    for f in range(channels):
        for copy in small[f]:
            copy.wait()
        if with_update:
            m = mv[f].reshape(multipoles, mv.shape[3])
            half = fv.shape[2] // 2
            for kb in range(blocks):
                beams[f][2 * kb].wait()
                beams[f][2 * kb + 1].wait()
                upper = jnp.dot(bv[f, pl.ds(kb * ROW_BLOCK, ROW_BLOCK)], m, preferred_element_type=jnp.float32)
                lower = jnp.dot(bv[f, pl.ds(modes + kb * ROW_BLOCK, ROW_BLOCK)], m, preferred_element_type=jnp.float32)
                image = jnp.concatenate(
                    [upper[:, :half] - lower[:, half:], upper[:, half:] + lower[:, :half]], axis=1
                )
                fld = fv[f, pl.ds(kb * ROW_BLOCK, ROW_BLOCK)]
                rhs = pv[f, pl.ds(kb * ROW_BLOCK, ROW_BLOCK)]
                noise = nv[f, pl.ds(kb * ROW_BLOCK, ROW_BLOCK)]
                fld_out[f, pl.ds(kb * ROW_BLOCK, ROW_BLOCK)] = fld + WEIGHT * (rhs - image - noise * fld)
            new = fld_out[f]
        else:
            for copy in beams[f]:
                copy.wait()
            new = fv[f]
        sky = jnp.dot(_stack_t(new), bv[f], preferred_element_type=jnp.float32)
        sky_out[:, f, :] = sky.T.astype(sky_out.dtype)


def sweep(beam_table, field, mixed=None, probes=None, noise=None):
    channels, rows, multipoles = beam_table.shape
    modes, columns = field.shape[1], field.shape[2]
    with_update = mixed is not None
    any_space = pl.BlockSpec(memory_space=pl.ANY)
    vmem = pl.BlockSpec(memory_space=pltpu.MemorySpace.VMEM)
    sky_shape = jax.ShapeDtypeStruct((multipoles, channels, columns), jnp.bfloat16)
    blocks = modes // ROW_BLOCK
    flops = 2 * channels * rows * multipoles * columns
    scratch = [pltpu.VMEM(beam_table.shape, beam_table.dtype), pltpu.VMEM(field.shape, jnp.float32)]
    if with_update:
        devices = mixed.shape[0]
        scratch = [
            pltpu.VMEM(beam_table.shape, beam_table.dtype),
            pltpu.VMEM((channels, devices, mixed.shape[2], mixed.shape[3]), mixed.dtype),
            pltpu.VMEM(field.shape, jnp.float32),
            pltpu.VMEM(field.shape, jnp.float32),
            pltpu.VMEM((channels, modes, 1), jnp.float32),
        ]
        n_sems = channels * (4 + 2 * blocks)
        in_specs = [any_space] * 5
        out_specs = [vmem, vmem]
        out_shape = [jax.ShapeDtypeStruct(field.shape, jnp.float32), sky_shape]
        args = (beam_table, mixed, field, probes, noise[:, :, None])
        flops *= 2
    else:
        n_sems = channels * (1 + 2 * blocks)
        in_specs = [any_space] * 2
        out_specs = vmem
        out_shape = sky_shape
        args = (beam_table, field)
    return pl.pallas_call(
        functools.partial(_sweep_kernel, with_update),
        in_specs=in_specs,
        out_specs=out_specs,
        out_shape=out_shape,
        scratch_shapes=scratch + [pltpu.SemaphoreType.DMA((n_sems,))],
        compiler_params=pltpu.CompilerParams(vmem_limit_bytes=56 * 1024 * 1024),
        cost_estimate=pl.CostEstimate(
            flops=flops, transcendentals=0, bytes_accessed=2 * channels * rows * multipoles + 12 * 1024 * 1024
        ),
    )(*args)


def to_multipoles(sky):
    return lax.all_to_all(sky, "chan", split_axis=0, concat_axis=1, tiled=True)


def mix(covariance, sky):
    channel_mixed = jnp.einsum("drj,dji->rdi", covariance, sky, preferred_element_type=jnp.float32)
    back = lax.all_to_all(channel_mixed.astype(jnp.bfloat16), "chan", split_axis=0, concat_axis=0, tiled=True)
    channels = back.shape[0]
    return back.reshape(channels // 2, 2, back.shape[1], back.shape[2])


def on_device(beam_table, covariance, noise_var, start_field, probes):
    column_entries = start_field.shape[2] // 2
    field = start_field
    sky = sweep(beam_table, field)
    for repeat in range(ITERS):
        mixed = mix(covariance, to_multipoles(sky))
        field, sky = sweep(beam_table, field, mixed, probes, noise_var)
    collected = to_multipoles(sky)
    multipole_band_power = (
        jnp.einsum("jmk,juk->jmu", collected, collected, preferred_element_type=jnp.float32) / column_entries
    )
    return (field, multipole_band_power.astype(jnp.bfloat16))


def solution(mesh):
    return jax.shard_map(
        on_device,
        mesh=mesh,
        in_specs=(
            P(("ma", "chan"), None, None),
            P(("ma", "chan"), None, None),
            P(("ma", "chan"), None),
            P(("ma", "chan"), None, None),
            P(("ma", "chan"), None, None),
        ),
        out_specs=(P(("ma", "chan"), None, None), P(("ma", "chan"), None, None)),
        check_vma=False,
    )
```

time: 364 us -> 339 us (0.931)
  blocking collectives: 176 us -> 232 us
  waiting for transfers between devices: 95.4 us -> 48.2 us
  Pallas kernels: 0 us -> 29.7 us
  matrix products: 33.6 us -> 5.05 us
  local copies, waits for them, and re-layouts: 40.8 us -> 15.7 us
  starting transfers between devices: 14 us -> 6.99 us
    all_to_all x3 -> x4, blocking collectives: 176 us -> 232 us  [the longest x3 176 us: to_multipoles(): return lax.all_to_all(sky, 'chan', split_axis=0, concat_axis=1, tiled=True)]
    all_to_all x2 -> x1, waiting for transfers between devices: 95.4 us -> 48.2 us  [mix(): lax.all_to_all(channel_mixed.astype(jnp.bfloat16), 'chan', split_axis=0,...]
    pallas_call x0 -> x3, Pallas kernels: none -> 29.7 us  [sweep(): pl.pallas_call(functools.partial(_sweep_kernel, with_update), in_specs=in...]
    dot_general x8 -> x3, matrix products: 33.6 us -> 5.05 us  [the longest x2 3.37 us: mix(): jnp.einsum('drj,dji->rdi', covariance, sky, preferred_element_type=jnp.fl...]
    convert_element_type x5 -> x2, local copies, waits for them, and re-layouts: 25.2 us -> 5.99 us  [mix(): channel_mixed.astype(jnp.bfloat16)]
    all_to_all x2 -> x1, starting transfers between devices: 14 us -> 6.99 us  [mix(): lax.all_to_all(channel_mixed.astype(jnp.bfloat16), 'chan', split_axis=0,...]
    unnamed x27 -> x6, local copies, waits for them, and re-layouts: 6.02 us -> 1.37 us
    all_to_all x9 -> x4, local copies, waits for them, and re-layouts: 9.61 us -> 7.27 us  [to_multipoles(): return lax.all_to_all(sky, 'chan', split_axis=0, concat_axis=1, tiled=True)]
  transfers between devices with their start and end apart: 2 -> 1, of which waited for: 2 -> 1; matrix products, arithmetic and copies ran while one was open for 1% -> 0% of each run, Pallas kernels for 0% -> 0%
where the time goes in v3:
time: 339 us; the launch traced here: 338 us
  blocking collectives  232 us (68%)
  waiting for transfers between devices  48.2 us (14%)
  Pallas kernels  29.7 us (9%)
  local copies, waits for them, and re-layouts  15.7 us (5%)
  starting transfers between devices  6.99 us (2%)
  matrix products  5.05 us (1%)
    all_to_all x3, blocking collectives, to_multipoles(): return lax.all_to_all(sky, 'chan', split_axis=0, concat_axis=1, tiled=True)  176 us
    all_to_all x1, blocking collectives, mix(): lax.all_to_all(channel_mixed.astype(jnp.bfloat16), 'chan', split_axis=0,...  56.1 us
    all_to_all x1, waiting for transfers between devices, mix(): lax.all_to_all(channel_mixed.astype(jnp.bfloat16), 'chan', split_axis=0,...  48.2 us
    pallas_call x3, Pallas kernels, sweep(): pl.pallas_call(functools.partial(_sweep_kernel, with_update), in_specs=in...  29.7 us
    all_to_all x4, local copies, waits for them, and re-layouts, to_multipoles(): return lax.all_to_all(sky, 'chan', split_axis=0, concat_axis=1, tiled=True)  7.27 us
    all_to_all x1, starting transfers between devices, mix(): lax.all_to_all(channel_mixed.astype(jnp.bfloat16), 'chan', split_axis=0,...  6.99 us
  transfers between devices with their start and end apart: 1, of which 1 were waited for; matrix products, arithmetic and copies ran while one was open for 0% of the time, Pallas kernels for 0%

profile of v3, /device:TPU:2, one launch (start us, length us, event | category | flops | bytes accessed | tf_op | source)
XLA Modules:
  0.0 338.0 jit_solution(16182034856386364002)
XLA Ops:
  0.6 0.0 copy-start
  0.6 8.2 %shard_map.68 = bf16[2048,2,256]{2,1,0:T(2,128)(2,1)} custom-call(bf16[2,1024,2048]{2,1,0:T(8,128)(2,1)} %refs_0_.5, f32[2,512,256]{2,1,0:T(8,128)} %refs_2_.1), custom_call_target="tpu_custom_call" | custom-call | flops 2147483648 | bytes 20971520 | tf_op jit(solution)/shard_map/pallas_call | solution.py:111
  8.8 63.4 %all_to_all.64 = bf16[2048,2,256]{2,1,0:T(2,128)(2,1)S(1)} all-to-all(bf16[2048,2,256]{2,1,0:T(2,128)(2,1)} %shard_map.68), channel_id=1, replica_groups=mesh['chan'=64,'ma'=4] {'chan'}, dimensions={0} | all-to-all | bytes 4194304 | tf_op jit(solution)/shard_map/all_to_all | solution.py:125
  72.2 0.5 copy.21
  72.7 0.0 copy-done
  72.7 1.7 convert_bitcast_fusion.1
  74.4 3.0 copy.23
  77.4 0.0 copy-start.2
  77.4 7.0 %all-to-all-start.1 = ((bf16[128,32,256]{2,1,0:T(8,128)(2,1)}), bf16[128,32,256]{2,1,0:T(8,128)(2,1)S(1)}, u32[]{:S(2)}, u32[]{:S(2)}) async-start(bf16[128,32,256]{2,1,0:T(8,128)(2,1)} %copy.23), calls=%async_computation.1 | async-start | bytes 4194304 | tf_op jit(solution)/shard_map/all_to_all | solution.py:130
  84.4 0.0 copy-done.2
  84.4 1.0 copy.24.refs_4_
  85.5 48.2 %all-to-all-done.1 = bf16[128,32,256]{2,1,0:T(8,128)(2,1)S(1)} async-done(((bf16[128,32,256]{2,1,0:T(8,128)(2,1)}), bf16[128,32,256]{2,1,0:T(8,128)(2,1)S(1)}, u32[]{:S(2)}, u32[]{:S(2)}) %all-to-all-start.1) | async-done | bytes 2097184 | tf_op jit(solution)/shard_map/all_to_all | solution.py:130
  133.7 0.0 copy-start.1
  133.7 1.4 copy-done.1
  135.1 10.7 %shard_map.69 = (f32[2,512,256]{2,1,0:T(8,128)}, bf16[2048,2,256]{2,1,0:T(2,128)(2,1)}) custom-call(bf16[2,1024,2048]{2,1,0:T(8,128)(2,1)} %refs_0_.5, bf16[64,2,32,256]{3,2,1,0:T(8,128)(2,1)} %bitcast.27, f32[2,512,256]{2,1,0:T(8,128)} %refs_2_.1, f32[2,512,256]{2,1,0:T(8,128)} %refs_3_.3, f32[2,512,1]{2,1,0:T(8,128)} %copy.24.refs_4_), custom_call_target="tpu_custom_call" | custom-call | flops 4294967296 | bytes 20971520 | tf_op jit(solution)/shard_map/pallas_call | solution.py:111
  145.8 56.1 %all_to_all.65 = bf16[2048,2,256]{2,1,0:T(2,128)(2,1)S(1)} all-to-all(bf16[2048,2,256]{2,1,0:T(2,128)(2,1)} %get-tuple-element.6), channel_id=1, replica_groups=mesh['chan'=64,'ma'=4] {'chan'}, dimensions={0} | all-to-all | bytes 4194304 | tf_op jit(solution)/shard_map/all_to_all | solution.py:125
  201.9 0.5 copy.25
  202.4 1.7 convert_bitcast_fusion
  204.1 3.0 copy.27
  207.1 56.1 %all_to_all.66 = bf16[128,32,256]{2,1,0:T(8,128)(2,1)} all-to-all(bf16[128,32,256]{2,1,0:T(8,128)(2,1)} %copy.27), channel_id=1, replica_groups=mesh['chan'=64,'ma'=4] {'chan'}, dimensions={0} | all-to-all | bytes 4194304 | tf_op jit(solution)/shard_map/all_to_all | solution.py:130
  263.2 10.7 %shard_map.70 = (f32[2,512,256]{2,1,0:T(8,128)}, bf16[2048,2,256]{2,1,0:T(2,128)(2,1)}) custom-call(bf16[2,1024,2048]{2,1,0:T(8,128)(2,1)} %refs_0_.5, bf16[64,2,32,256]{3,2,1,0:T(8,128)(2,1)} %bitcast.28, f32[2,512,256]{2,1,0:T(8,128)} %get-tuple-element.7.refs_2_, f32[2,512,256]{2,1,0:T(8,128)} %refs_3_.3, f32[2,512,1]{2,1,0:T(8,128)} %copy.24.refs_4_), custom_call_target="tpu_custom_call" | custom-call | flops 4294967296 | bytes 20971520 | tf_op jit(solution)/shard_map/pallas_call | solution.py:111
  273.9 56.0 %all_to_all.67 = bf16[2048,2,256]{2,1,0:T(2,128)(2,1)S(1)} all-to-all(bf16[2048,2,256]{2,1,0:T(2,128)(2,1)} %get-tuple-element.9), channel_id=1, replica_groups=mesh['chan'=64,'ma'=4] {'chan'}, dimensions={0} | all-to-all | bytes 4194304 | tf_op jit(solution)/shard_map/all_to_all | solution.py:125
  330.0 3.6 %copy.29 = bf16[32,64,2,256]{3,2,1,0:T(2,128)(2,1)} copy(bf16[32,64,2,256]{3,2,0,1:T(2,128)(2,1)S(1)} %bitcast.26) | data formatting | bytes 4194304 | tf_op jit(solution)/shard_map/all_to_all | solution.py:125
  333.5 2.7 all_to_all.58
  336.3 1.7 multiply_convert_fusion
Async XLA Ops:
  0.6 72.1 %copy-start = (bf16[32,128,128]{2,1,0:T(8,128)(2,1)S(1)}, bf16[32,128,128]{2,1,0:T(8,128)(2,1)}, u32[]{:S(2)}) copy-start(bf16[32,128,128]{2,1,0:T(8,128)(2,1)} %param.6) | copy-start | bytes 3145732
  77.4 7.0 %copy-start.2 = (f32[2,512]{1,0:T(2,128)S(1)}, f32[2,512]{1,0:T(2,128)}, u32[]{:S(2)}) copy-start(f32[2,512]{1,0:T(2,128)} %param.7) | copy-start | bytes 12292
  77.4 56.3 %all-to-all-start.1 = ((bf16[128,32,256]{2,1,0:T(8,128)(2,1)}), bf16[128,32,256]{2,1,0:T(8,128)(2,1)S(1)}, u32[]{:S(2)}, u32[]{:S(2)}) async-start(bf16[128,32,256]{2,1,0:T(8,128)(2,1)} %copy.23), calls=%async_computation.1 | async-start | bytes 4194304 | tf_op jit(solution)/shard_map/all_to_all | solution.py:130
  133.7 1.4 copy-start.1

commit v4 on v3

--- a/solution.py
+++ b/solution.py
@@ -10,6 +10,7 @@
 ITERS = 2
 WEIGHT = 0.2
 ROW_BLOCK = 256
+L_BLOCK = 512
 
 
 def _stack_t(new):
@@ -24,9 +25,9 @@
 
 def _sweep_kernel(with_update, *refs):
     if with_update:
-        b_hbm, m_hbm, f_hbm, p_hbm, n_hbm, fld_out, sky_out, bv, mv, fv, pv, nv, sems = refs
+        b_hbm, m_hbm, f_hbm, p_hbm, n_hbm, fld_out, sky_out, bv, mv, fv, pv, nv, gv, sv, sems = refs
     else:
-        b_hbm, f_hbm, sky_out, bv, fv, sems = refs
+        b_hbm, f_hbm, sky_out, bv, fv, sv, sems = refs
     channels, rows, multipoles = bv.shape
     modes = fv.shape[1]
     blocks = modes // ROW_BLOCK
@@ -37,7 +38,7 @@
         copy.start()
         return copy
 
-    small, beams = [], []
+    small, beams, outgoing = [], [], []
     for f in range(channels):
         group = [start(f_hbm.at[f], fv.at[f])]
         if with_update:
@@ -64,17 +65,23 @@
                 image = jnp.concatenate(
                     [upper[:, :half] - lower[:, half:], upper[:, half:] + lower[:, :half]], axis=1
                 )
-                fld = fv[f, pl.ds(kb * ROW_BLOCK, ROW_BLOCK)]
-                rhs = pv[f, pl.ds(kb * ROW_BLOCK, ROW_BLOCK)]
-                noise = nv[f, pl.ds(kb * ROW_BLOCK, ROW_BLOCK)]
-                fld_out[f, pl.ds(kb * ROW_BLOCK, ROW_BLOCK)] = fld + WEIGHT * (rhs - image - noise * fld)
-            new = fld_out[f]
+                block = pl.ds(kb * ROW_BLOCK, ROW_BLOCK)
+                fld = fv[f, block]
+                gv[f, block] = fld + WEIGHT * (pv[f, block] - image - nv[f, block] * fld)
+                outgoing.append(start(gv.at[f, block], fld_out.at[f, block]))
+            stacked_t = _stack_t(gv[f])
         else:
             for copy in beams[f]:
                 copy.wait()
-            new = fv[f]
-        sky = jnp.dot(_stack_t(new), bv[f], preferred_element_type=jnp.float32)
-        sky_out[:, f, :] = sky.T.astype(sky_out.dtype)
+            stacked_t = _stack_t(fv[f])
+        for lb in range(multipoles // L_BLOCK):
+            cols = pl.ds(lb * L_BLOCK, L_BLOCK)
+            sky = jnp.dot(stacked_t, bv[f, :, cols], preferred_element_type=jnp.float32)
+            sv[cols, f, :] = sky.T.astype(sv.dtype)
+            if f == channels - 1:
+                outgoing.append(start(sv.at[cols], sky_out.at[cols]))
+    for copy in outgoing:
+        copy.wait()
 
 
 def sweep(beam_table, field, mixed=None, probes=None, noise=None):
@@ -82,11 +89,11 @@
     modes, columns = field.shape[1], field.shape[2]
     with_update = mixed is not None
     any_space = pl.BlockSpec(memory_space=pl.ANY)
-    vmem = pl.BlockSpec(memory_space=pltpu.MemorySpace.VMEM)
     sky_shape = jax.ShapeDtypeStruct((multipoles, channels, columns), jnp.bfloat16)
     blocks = modes // ROW_BLOCK
     flops = 2 * channels * rows * multipoles * columns
-    scratch = [pltpu.VMEM(beam_table.shape, beam_table.dtype), pltpu.VMEM(field.shape, jnp.float32)]
+    sky_scratch = pltpu.VMEM((multipoles, channels, columns), jnp.bfloat16)
+    scratch = [pltpu.VMEM(beam_table.shape, beam_table.dtype), pltpu.VMEM(field.shape, jnp.float32), sky_scratch]
     if with_update:
         devices = mixed.shape[0]
         scratch = [
@@ -95,17 +102,19 @@
             pltpu.VMEM(field.shape, jnp.float32),
             pltpu.VMEM(field.shape, jnp.float32),
             pltpu.VMEM((channels, modes, 1), jnp.float32),
+            pltpu.VMEM(field.shape, jnp.float32),
+            sky_scratch,
         ]
-        n_sems = channels * (4 + 2 * blocks)
+        n_sems = channels * (4 + 3 * blocks) + multipoles // L_BLOCK
         in_specs = [any_space] * 5
-        out_specs = [vmem, vmem]
+        out_specs = [any_space, any_space]
         out_shape = [jax.ShapeDtypeStruct(field.shape, jnp.float32), sky_shape]
         args = (beam_table, mixed, field, probes, noise[:, :, None])
         flops *= 2
     else:
-        n_sems = channels * (1 + 2 * blocks)
+        n_sems = channels * (1 + 2 * blocks) + multipoles // L_BLOCK
         in_specs = [any_space] * 2
-        out_specs = vmem
+        out_specs = any_space
         out_shape = sky_shape
         args = (beam_table, field)
     return pl.pallas_call(

time: 339 us -> 337 us (level)
  no operation moved by 1% of the time
where the time goes in v4:
time: 337 us; the launch traced here: 336 us
  blocking collectives  232 us (69%)
  waiting for transfers between devices  48.2 us (14%)
  Pallas kernels  28.2 us (8%)
  local copies, waits for them, and re-layouts  15.7 us (5%)
  starting transfers between devices  6.99 us (2%)
  matrix products  5.04 us (1%)
    all_to_all x3, blocking collectives, to_multipoles(): return lax.all_to_all(sky, 'chan', split_axis=0, concat_axis=1, tiled=True)  175 us
    all_to_all x1, blocking collectives, mix(): lax.all_to_all(channel_mixed.astype(jnp.bfloat16), 'chan', split_axis=0,...  56.1 us
    all_to_all x1, waiting for transfers between devices, mix(): lax.all_to_all(channel_mixed.astype(jnp.bfloat16), 'chan', split_axis=0,...  48.2 us
    pallas_call x3, Pallas kernels, sweep(): pl.pallas_call(functools.partial(_sweep_kernel, with_update), in_specs=in...  28.2 us
    all_to_all x4, local copies, waits for them, and re-layouts, to_multipoles(): return lax.all_to_all(sky, 'chan', split_axis=0, concat_axis=1, tiled=True)  7.27 us
    all_to_all x1, starting transfers between devices, mix(): lax.all_to_all(channel_mixed.astype(jnp.bfloat16), 'chan', split_axis=0,...  6.99 us
  transfers between devices with their start and end apart: 1, of which 1 were waited for; matrix products, arithmetic and copies ran while one was open for 0% of the time, Pallas kernels for 0%

profile of v4, /device:TPU:2, one launch (start us, length us, event | category | flops | bytes accessed | tf_op | source)
XLA Modules:
  0.0 336.5 jit_solution(3832733469733627049)
XLA Ops:
  0.6 0.0 copy-start
  0.6 7.6 %shard_map.68 = bf16[2048,2,256]{2,1,0:T(2,128)(2,1)} custom-call(bf16[2,1024,2048]{2,1,0:T(8,128)(2,1)} %refs_0_.5, f32[2,512,256]{2,1,0:T(8,128)} %refs_2_.1), custom_call_target="tpu_custom_call" | custom-call | flops 2147483648 | bytes 20971520 | tf_op jit(solution)/shard_map/pallas_call | solution.py:120
  8.3 63.4 %all_to_all.64 = bf16[2048,2,256]{2,1,0:T(2,128)(2,1)S(1)} all-to-all(bf16[2048,2,256]{2,1,0:T(2,128)(2,1)} %shard_map.68), channel_id=1, replica_groups=mesh['chan'=64,'ma'=4] {'chan'}, dimensions={0} | all-to-all | bytes 4194304 | tf_op jit(solution)/shard_map/all_to_all | solution.py:134
  71.7 0.5 copy.21
  72.2 0.0 copy-done
  72.2 1.7 convert_bitcast_fusion.1
  73.9 3.0 copy.23
  76.9 0.0 copy-start.2
  76.9 7.0 %all-to-all-start.1 = ((bf16[128,32,256]{2,1,0:T(8,128)(2,1)}), bf16[128,32,256]{2,1,0:T(8,128)(2,1)S(1)}, u32[]{:S(2)}, u32[]{:S(2)}) async-start(bf16[128,32,256]{2,1,0:T(8,128)(2,1)} %copy.23), calls=%async_computation.1 | async-start | bytes 4194304 | tf_op jit(solution)/shard_map/all_to_all | solution.py:139
  83.9 0.0 copy-done.2
  83.9 1.0 copy.24.refs_4_
  85.0 48.2 %all-to-all-done.1 = bf16[128,32,256]{2,1,0:T(8,128)(2,1)S(1)} async-done(((bf16[128,32,256]{2,1,0:T(8,128)(2,1)}), bf16[128,32,256]{2,1,0:T(8,128)(2,1)S(1)}, u32[]{:S(2)}, u32[]{:S(2)}) %all-to-all-start.1) | async-done | bytes 2097184 | tf_op jit(solution)/shard_map/all_to_all | solution.py:139
  133.2 0.0 copy-start.1
  133.2 1.4 copy-done.1
  134.6 10.3 %shard_map.69 = (f32[2,512,256]{2,1,0:T(8,128)}, bf16[2048,2,256]{2,1,0:T(2,128)(2,1)}) custom-call(bf16[2,1024,2048]{2,1,0:T(8,128)(2,1)} %refs_0_.5, bf16[64,2,32,256]{3,2,1,0:T(8,128)(2,1)} %bitcast.27, f32[2,512,256]{2,1,0:T(8,128)} %refs_2_.1, f32[2,512,256]{2,1,0:T(8,128)} %refs_3_.3, f32[2,512,1]{2,1,0:T(8,128)} %copy.24.refs_4_), custom_call_target="tpu_custom_call" | custom-call | flops 4294967296 | bytes 20971520 | tf_op jit(solution)/shard_map/pallas_call | solution.py:120
  144.9 56.1 %all_to_all.65 = bf16[2048,2,256]{2,1,0:T(2,128)(2,1)S(1)} all-to-all(bf16[2048,2,256]{2,1,0:T(2,128)(2,1)} %get-tuple-element.6), channel_id=1, replica_groups=mesh['chan'=64,'ma'=4] {'chan'}, dimensions={0} | all-to-all | bytes 4194304 | tf_op jit(solution)/shard_map/all_to_all | solution.py:134
  200.9 0.5 copy.25
  201.4 1.7 convert_bitcast_fusion
  203.1 3.0 copy.27
  206.1 56.1 %all_to_all.66 = bf16[128,32,256]{2,1,0:T(8,128)(2,1)} all-to-all(bf16[128,32,256]{2,1,0:T(8,128)(2,1)} %copy.27), channel_id=1, replica_groups=mesh['chan'=64,'ma'=4] {'chan'}, dimensions={0} | all-to-all | bytes 4194304 | tf_op jit(solution)/shard_map/all_to_all | solution.py:139
  262.2 10.3 %shard_map.70 = (f32[2,512,256]{2,1,0:T(8,128)}, bf16[2048,2,256]{2,1,0:T(2,128)(2,1)}) custom-call(bf16[2,1024,2048]{2,1,0:T(8,128)(2,1)} %refs_0_.5, bf16[64,2,32,256]{3,2,1,0:T(8,128)(2,1)} %bitcast.28, f32[2,512,256]{2,1,0:T(8,128)} %get-tuple-element.7.refs_2_, f32[2,512,256]{2,1,0:T(8,128)} %refs_3_.3, f32[2,512,1]{2,1,0:T(8,128)} %copy.24.refs_4_), custom_call_target="tpu_custom_call" | custom-call | flops 4294967296 | bytes 20971520 | tf_op jit(solution)/shard_map/pallas_call | solution.py:120
  272.5 56.0 %all_to_all.67 = bf16[2048,2,256]{2,1,0:T(2,128)(2,1)S(1)} all-to-all(bf16[2048,2,256]{2,1,0:T(2,128)(2,1)} %get-tuple-element.9), channel_id=1, replica_groups=mesh['chan'=64,'ma'=4] {'chan'}, dimensions={0} | all-to-all | bytes 4194304 | tf_op jit(solution)/shard_map/all_to_all | solution.py:134
  328.4 3.6 %copy.29 = bf16[32,64,2,256]{3,2,1,0:T(2,128)(2,1)} copy(bf16[32,64,2,256]{3,2,0,1:T(2,128)(2,1)S(1)} %bitcast.26) | data formatting | bytes 4194304 | tf_op jit(solution)/shard_map/all_to_all | solution.py:134
  332.0 2.7 all_to_all.58
  334.8 1.7 multiply_convert_fusion
Async XLA Ops:
  0.6 71.6 %copy-start = (bf16[32,128,128]{2,1,0:T(8,128)(2,1)S(1)}, bf16[32,128,128]{2,1,0:T(8,128)(2,1)}, u32[]{:S(2)}) copy-start(bf16[32,128,128]{2,1,0:T(8,128)(2,1)} %param.6) | copy-start | bytes 3145732
  76.9 7.0 %copy-start.2 = (f32[2,512]{1,0:T(2,128)S(1)}, f32[2,512]{1,0:T(2,128)}, u32[]{:S(2)}) copy-start(f32[2,512]{1,0:T(2,128)} %param.7) | copy-start | bytes 12292
  76.9 56.3 %all-to-all-start.1 = ((bf16[128,32,256]{2,1,0:T(8,128)(2,1)}), bf16[128,32,256]{2,1,0:T(8,128)(2,1)S(1)}, u32[]{:S(2)}, u32[]{:S(2)}) async-start(bf16[128,32,256]{2,1,0:T(8,128)(2,1)} %copy.23), calls=%async_computation.1 | async-start | bytes 4194304 | tf_op jit(solution)/shard_map/all_to_all | solution.py:139
  133.2 1.4 copy-start.1

commit v5 on v4

--- a/solution.py
+++ b/solution.py
@@ -25,7 +25,7 @@
 
 def _sweep_kernel(with_update, *refs):
     if with_update:
-        b_hbm, m_hbm, f_hbm, p_hbm, n_hbm, fld_out, sky_out, bv, mv, fv, pv, nv, gv, sv, sems = refs
+        b_hbm, m_hbm, f_hbm, p_hbm, n_hbm, fld_out, sky_out, bv, mv, fv, pv, gv, sv, sems = refs
     else:
         b_hbm, f_hbm, sky_out, bv, fv, sv, sems = refs
     channels, rows, multipoles = bv.shape
@@ -42,7 +42,7 @@
     for f in range(channels):
         group = [start(f_hbm.at[f], fv.at[f])]
         if with_update:
-            group += [start(m_hbm.at[:, f], mv.at[f]), start(p_hbm.at[f], pv.at[f]), start(n_hbm.at[f], nv.at[f])]
+            group += [start(m_hbm.at[:, f], mv.at[f]), start(p_hbm.at[f], pv.at[f])]
         small.append(group)
         parts = []
         for kb in range(blocks):
@@ -56,6 +56,8 @@
             copy.wait()
         if with_update:
             m = mv[f].reshape(multipoles, mv.shape[3])
+            noise_row = n_hbm[pl.ds(f, 1), :]
+            noise_col = jnp.broadcast_to(noise_row, (128, modes)).T[:, :1]
             half = fv.shape[2] // 2
             for kb in range(blocks):
                 beams[f][2 * kb].wait()
@@ -67,7 +69,7 @@
                 )
                 block = pl.ds(kb * ROW_BLOCK, ROW_BLOCK)
                 fld = fv[f, block]
-                gv[f, block] = fld + WEIGHT * (pv[f, block] - image - nv[f, block] * fld)
+                gv[f, block] = fld + WEIGHT * (pv[f, block] - image - noise_col[kb * ROW_BLOCK:(kb + 1) * ROW_BLOCK] * fld)
                 outgoing.append(start(gv.at[f, block], fld_out.at[f, block]))
             stacked_t = _stack_t(gv[f])
         else:
@@ -101,15 +103,14 @@
             pltpu.VMEM((channels, devices, mixed.shape[2], mixed.shape[3]), mixed.dtype),
             pltpu.VMEM(field.shape, jnp.float32),
             pltpu.VMEM(field.shape, jnp.float32),
-            pltpu.VMEM((channels, modes, 1), jnp.float32),
             pltpu.VMEM(field.shape, jnp.float32),
             sky_scratch,
         ]
-        n_sems = channels * (4 + 3 * blocks) + multipoles // L_BLOCK
-        in_specs = [any_space] * 5
+        n_sems = channels * (3 + 3 * blocks) + multipoles // L_BLOCK
+        in_specs = [any_space] * 4 + [pl.BlockSpec(memory_space=pltpu.MemorySpace.VMEM)]
         out_specs = [any_space, any_space]
         out_shape = [jax.ShapeDtypeStruct(field.shape, jnp.float32), sky_shape]
-        args = (beam_table, mixed, field, probes, noise[:, :, None])
+        args = (beam_table, mixed, field, probes, noise)
         flops *= 2
     else:
         n_sems = channels * (1 + 2 * blocks) + multipoles // L_BLOCK

time: 337 us -> 337 us (level)
  blocking collectives: 232 us -> 288 us
  waiting for transfers between devices: 48.2 us -> 0 us
  starting transfers between devices: 6.99 us -> 0 us
    all_to_all x1 -> x2, blocking collectives: 56.1 us -> 112 us  [mix(): lax.all_to_all(channel_mixed.astype(jnp.bfloat16), 'chan', split_axis=0,...]
    all_to_all x1 -> x0, waiting for transfers between devices: 48.2 us -> none  [mix(): lax.all_to_all(channel_mixed.astype(jnp.bfloat16), 'chan', split_axis=0,...]
    all_to_all x1 -> x0, starting transfers between devices: 6.99 us -> none  [mix(): lax.all_to_all(channel_mixed.astype(jnp.bfloat16), 'chan', split_axis=0,...]
  transfers between devices with their start and end apart: 1 -> 0, of which waited for: 1 -> 0; matrix products, arithmetic and copies ran while one was open for 0% -> 0% of each run, Pallas kernels for 0% -> 0%
where the time goes in v5:
time: 337 us; the launch traced here: 336 us
  blocking collectives  288 us (85%)
  Pallas kernels  29.6 us (9%)
  local copies, waits for them, and re-layouts  13.2 us (4%)
  matrix products  5.05 us (1%)
    all_to_all x3, blocking collectives, to_multipoles(): return lax.all_to_all(sky, 'chan', split_axis=0, concat_axis=1, tiled=True)  175 us
    all_to_all x2, blocking collectives, mix(): lax.all_to_all(channel_mixed.astype(jnp.bfloat16), 'chan', split_axis=0,...  112 us
    pallas_call x3, Pallas kernels, sweep(): pl.pallas_call(functools.partial(_sweep_kernel, with_update), in_specs=in...  29.6 us
    all_to_all x4, local copies, waits for them, and re-layouts, to_multipoles(): return lax.all_to_all(sky, 'chan', split_axis=0, concat_axis=1, tiled=True)  7.25 us

profile of v5, /device:TPU:2, one launch (start us, length us, event | category | flops | bytes accessed | tf_op | source)
XLA Modules:
  0.0 336.4 jit_solution(3283272980334779970)
XLA Ops:
  0.6 0.0 copy-start
  0.6 7.6 %shard_map.68 = bf16[2048,2,256]{2,1,0:T(2,128)(2,1)} custom-call(bf16[2,1024,2048]{2,1,0:T(8,128)(2,1)} %refs_0_.5, f32[2,512,256]{2,1,0:T(8,128)} %refs_2_.1), custom_call_target="tpu_custom_call" | custom-call | flops 2147483648 | bytes 20971520 | tf_op jit(solution)/shard_map/pallas_call | solution.py:121
  8.3 63.4 %all_to_all.64 = bf16[2048,2,256]{2,1,0:T(2,128)(2,1)S(1)} all-to-all(bf16[2048,2,256]{2,1,0:T(2,128)(2,1)} %shard_map.68), channel_id=1, replica_groups=mesh['chan'=64,'ma'=4] {'chan'}, dimensions={0} | all-to-all | bytes 4194304 | tf_op jit(solution)/shard_map/all_to_all | solution.py:135
  71.7 0.5 copy.19
  72.2 0.0 copy-done
  72.2 1.7 convert_bitcast_fusion.1
  73.9 3.0 copy.21
  76.8 56.2 %all_to_all.65 = bf16[128,32,256]{2,1,0:T(8,128)(2,1)} all-to-all(bf16[128,32,256]{2,1,0:T(8,128)(2,1)} %copy.21), channel_id=1, replica_groups=mesh['chan'=64,'ma'=4] {'chan'}, dimensions={0} | all-to-all | bytes 4194304 | tf_op jit(solution)/shard_map/all_to_all | solution.py:140
  133.1 11.0 %shard_map.69 = (f32[2,512,256]{2,1,0:T(8,128)}, bf16[2048,2,256]{2,1,0:T(2,128)(2,1)}) custom-call(bf16[2,1024,2048]{2,1,0:T(8,128)(2,1)} %refs_0_.5, bf16[64,2,32,256]{3,2,1,0:T(8,128)(2,1)} %bitcast.27, f32[2,512,256]{2,1,0:T(8,128)} %refs_2_.1, f32[2,512,256]{2,1,0:T(8,128)} %refs_3_.3, f32[2,512]{1,0:T(2,128)} %refs_4_.3), custom_call_target="tpu_custom_call" | custom-call | flops 4294967296 | bytes 20971520 | tf_op jit(solution)/shard_map/pallas_call | solution.py:121
  144.1 56.1 %all_to_all.66 = bf16[2048,2,256]{2,1,0:T(2,128)(2,1)S(1)} all-to-all(bf16[2048,2,256]{2,1,0:T(2,128)(2,1)} %get-tuple-element.6), channel_id=1, replica_groups=mesh['chan'=64,'ma'=4] {'chan'}, dimensions={0} | all-to-all | bytes 4194304 | tf_op jit(solution)/shard_map/all_to_all | solution.py:135
  200.2 0.5 copy.22
  200.7 1.7 convert_bitcast_fusion
  202.4 3.0 copy.24
  205.3 56.1 %all_to_all.67 = bf16[128,32,256]{2,1,0:T(8,128)(2,1)} all-to-all(bf16[128,32,256]{2,1,0:T(8,128)(2,1)} %copy.24), channel_id=1, replica_groups=mesh['chan'=64,'ma'=4] {'chan'}, dimensions={0} | all-to-all | bytes 4194304 | tf_op jit(solution)/shard_map/all_to_all | solution.py:140
  261.4 11.0 %shard_map.70 = (f32[2,512,256]{2,1,0:T(8,128)}, bf16[2048,2,256]{2,1,0:T(2,128)(2,1)}) custom-call(bf16[2,1024,2048]{2,1,0:T(8,128)(2,1)} %refs_0_.5, bf16[64,2,32,256]{3,2,1,0:T(8,128)(2,1)} %bitcast.26, f32[2,512,256]{2,1,0:T(8,128)} %get-tuple-element.7.refs_2_, f32[2,512,256]{2,1,0:T(8,128)} %refs_3_.3, f32[2,512]{1,0:T(2,128)} %refs_4_.3), custom_call_target="tpu_custom_call" | custom-call | flops 4294967296 | bytes 20971520 | tf_op jit(solution)/shard_map/pallas_call | solution.py:121
  272.4 56.0 %all_to_all.68 = bf16[2048,2,256]{2,1,0:T(2,128)(2,1)S(1)} all-to-all(bf16[2048,2,256]{2,1,0:T(2,128)(2,1)} %get-tuple-element.9), channel_id=1, replica_groups=mesh['chan'=64,'ma'=4] {'chan'}, dimensions={0} | all-to-all | bytes 4194304 | tf_op jit(solution)/shard_map/all_to_all | solution.py:135
  328.4 3.6 %copy.25 = bf16[32,64,2,256]{3,2,1,0:T(2,128)(2,1)} copy(bf16[32,64,2,256]{3,2,0,1:T(2,128)(2,1)S(1)} %bitcast.25) | data formatting | bytes 4194304 | tf_op jit(solution)/shard_map/all_to_all | solution.py:135
  332.0 2.7 all_to_all.58
  334.7 1.7 multiply_convert_fusion
Async XLA Ops:
  0.6 71.6 %copy-start = (bf16[32,128,128]{2,1,0:T(8,128)(2,1)S(1)}, bf16[32,128,128]{2,1,0:T(8,128)(2,1)}, u32[]{:S(2)}) copy-start(bf16[32,128,128]{2,1,0:T(8,128)(2,1)} %param.6) | copy-start | bytes 3145732

commit v6 on v5

--- a/solution.py
+++ b/solution.py
@@ -25,7 +25,7 @@
 
 def _sweep_kernel(with_update, *refs):
     if with_update:
-        b_hbm, m_hbm, f_hbm, p_hbm, n_hbm, fld_out, sky_out, bv, mv, fv, pv, gv, sv, sems = refs
+        b_hbm, m_hbm, f_hbm, p_hbm, n_hbm, fld_out, sky_out, bv, mv, fv, pv, nv, gv, sv, sems = refs
     else:
         b_hbm, f_hbm, sky_out, bv, fv, sv, sems = refs
     channels, rows, multipoles = bv.shape
@@ -43,6 +43,8 @@
         group = [start(f_hbm.at[f], fv.at[f])]
         if with_update:
             group += [start(m_hbm.at[:, f], mv.at[f]), start(p_hbm.at[f], pv.at[f])]
+            if f == 0:
+                group.append(start(n_hbm, nv))
         small.append(group)
         parts = []
         for kb in range(blocks):
@@ -56,7 +58,7 @@
             copy.wait()
         if with_update:
             m = mv[f].reshape(multipoles, mv.shape[3])
-            noise_row = n_hbm[pl.ds(f, 1), :]
+            noise_row = nv[pl.ds(f, 1), :]
             noise_col = jnp.broadcast_to(noise_row, (128, modes)).T[:, :1]
             half = fv.shape[2] // 2
             for kb in range(blocks):
@@ -103,11 +105,12 @@
             pltpu.VMEM((channels, devices, mixed.shape[2], mixed.shape[3]), mixed.dtype),
             pltpu.VMEM(field.shape, jnp.float32),
             pltpu.VMEM(field.shape, jnp.float32),
+            pltpu.VMEM(noise.shape, jnp.float32),
             pltpu.VMEM(field.shape, jnp.float32),
             sky_scratch,
         ]
-        n_sems = channels * (3 + 3 * blocks) + multipoles // L_BLOCK
-        in_specs = [any_space] * 4 + [pl.BlockSpec(memory_space=pltpu.MemorySpace.VMEM)]
+        n_sems = channels * (3 + 3 * blocks) + 1 + multipoles // L_BLOCK
+        in_specs = [any_space] * 5
         out_specs = [any_space, any_space]
         out_shape = [jax.ShapeDtypeStruct(field.shape, jnp.float32), sky_shape]
         args = (beam_table, mixed, field, probes, noise)

time: 337 us -> 336 us (level)
  no operation moved by 1% of the time
where the time goes in v6:
time: 336 us; the launch traced here: 335 us
  blocking collectives  288 us (86%)
  Pallas kernels  28.3 us (8%)
  local copies, waits for them, and re-layouts  13.2 us (4%)
  matrix products  5.04 us (2%)
    all_to_all x3, blocking collectives, to_multipoles(): return lax.all_to_all(sky, 'chan', split_axis=0, concat_axis=1, tiled=True)  175 us
    all_to_all x2, blocking collectives, mix(): lax.all_to_all(channel_mixed.astype(jnp.bfloat16), 'chan', split_axis=0,...  112 us
    pallas_call x3, Pallas kernels, sweep(): pl.pallas_call(functools.partial(_sweep_kernel, with_update), in_specs=in...  28.3 us
    all_to_all x4, local copies, waits for them, and re-layouts, to_multipoles(): return lax.all_to_all(sky, 'chan', split_axis=0, concat_axis=1, tiled=True)  7.25 us

profile of v6, /device:TPU:2, one launch (start us, length us, event | category | flops | bytes accessed | tf_op | source)
XLA Modules:
  0.0 335.1 jit_solution(11614830786458589774)
XLA Ops:
  0.6 0.0 copy-start
  0.6 7.6 %shard_map.68 = bf16[2048,2,256]{2,1,0:T(2,128)(2,1)} custom-call(bf16[2,1024,2048]{2,1,0:T(8,128)(2,1)} %refs_0_.5, f32[2,512,256]{2,1,0:T(8,128)} %refs_2_.1), custom_call_target="tpu_custom_call" | custom-call | flops 2147483648 | bytes 20971520 | tf_op jit(solution)/shard_map/pallas_call | solution.py:124
  8.3 63.4 %all_to_all.64 = bf16[2048,2,256]{2,1,0:T(2,128)(2,1)S(1)} all-to-all(bf16[2048,2,256]{2,1,0:T(2,128)(2,1)} %shard_map.68), channel_id=1, replica_groups=mesh['chan'=64,'ma'=4] {'chan'}, dimensions={0} | all-to-all | bytes 4194304 | tf_op jit(solution)/shard_map/all_to_all | solution.py:138
  71.7 0.5 copy.19
  72.2 0.0 copy-done
  72.2 1.7 convert_bitcast_fusion.1
  73.9 3.0 copy.21
  76.8 56.2 %all_to_all.65 = bf16[128,32,256]{2,1,0:T(8,128)(2,1)} all-to-all(bf16[128,32,256]{2,1,0:T(8,128)(2,1)} %copy.21), channel_id=1, replica_groups=mesh['chan'=64,'ma'=4] {'chan'}, dimensions={0} | all-to-all | bytes 4194304 | tf_op jit(solution)/shard_map/all_to_all | solution.py:143
  133.1 10.4 %shard_map.69 = (f32[2,512,256]{2,1,0:T(8,128)}, bf16[2048,2,256]{2,1,0:T(2,128)(2,1)}) custom-call(bf16[2,1024,2048]{2,1,0:T(8,128)(2,1)} %refs_0_.5, bf16[64,2,32,256]{3,2,1,0:T(8,128)(2,1)} %bitcast.27, f32[2,512,256]{2,1,0:T(8,128)} %refs_2_.1, f32[2,512,256]{2,1,0:T(8,128)} %refs_3_.3, f32[2,512]{1,0:T(2,128)} %refs_4_.3), custom_call_target="tpu_custom_call" | custom-call | flops 4294967296 | bytes 20971520 | tf_op jit(solution)/shard_map/pallas_call | solution.py:124
  143.5 56.1 %all_to_all.66 = bf16[2048,2,256]{2,1,0:T(2,128)(2,1)S(1)} all-to-all(bf16[2048,2,256]{2,1,0:T(2,128)(2,1)} %get-tuple-element.6), channel_id=1, replica_groups=mesh['chan'=64,'ma'=4] {'chan'}, dimensions={0} | all-to-all | bytes 4194304 | tf_op jit(solution)/shard_map/all_to_all | solution.py:138
  199.5 0.5 copy.22
  200.0 1.7 convert_bitcast_fusion
  201.7 3.0 copy.24
  204.7 56.1 %all_to_all.67 = bf16[128,32,256]{2,1,0:T(8,128)(2,1)} all-to-all(bf16[128,32,256]{2,1,0:T(8,128)(2,1)} %copy.24), channel_id=1, replica_groups=mesh['chan'=64,'ma'=4] {'chan'}, dimensions={0} | all-to-all | bytes 4194304 | tf_op jit(solution)/shard_map/all_to_all | solution.py:143
  260.8 10.4 %shard_map.70 = (f32[2,512,256]{2,1,0:T(8,128)}, bf16[2048,2,256]{2,1,0:T(2,128)(2,1)}) custom-call(bf16[2,1024,2048]{2,1,0:T(8,128)(2,1)} %refs_0_.5, bf16[64,2,32,256]{3,2,1,0:T(8,128)(2,1)} %bitcast.26, f32[2,512,256]{2,1,0:T(8,128)} %get-tuple-element.7.refs_2_, f32[2,512,256]{2,1,0:T(8,128)} %refs_3_.3, f32[2,512]{1,0:T(2,128)} %refs_4_.3), custom_call_target="tpu_custom_call" | custom-call | flops 4294967296 | bytes 20971520 | tf_op jit(solution)/shard_map/pallas_call | solution.py:124
  271.2 56.0 %all_to_all.68 = bf16[2048,2,256]{2,1,0:T(2,128)(2,1)S(1)} all-to-all(bf16[2048,2,256]{2,1,0:T(2,128)(2,1)} %get-tuple-element.9), channel_id=1, replica_groups=mesh['chan'=64,'ma'=4] {'chan'}, dimensions={0} | all-to-all | bytes 4194304 | tf_op jit(solution)/shard_map/all_to_all | solution.py:138
  327.2 3.6 %copy.25 = bf16[32,64,2,256]{3,2,1,0:T(2,128)(2,1)} copy(bf16[32,64,2,256]{3,2,0,1:T(2,128)(2,1)S(1)} %bitcast.25) | data formatting | bytes 4194304 | tf_op jit(solution)/shard_map/all_to_all | solution.py:138
  330.7 2.7 all_to_all.58
  333.5 1.7 multiply_convert_fusion
Async XLA Ops:
  0.6 71.6 %copy-start = (bf16[32,128,128]{2,1,0:T(8,128)(2,1)S(1)}, bf16[32,128,128]{2,1,0:T(8,128)(2,1)}, u32[]{:S(2)}) copy-start(bf16[32,128,128]{2,1,0:T(8,128)(2,1)} %param.6) | copy-start | bytes 3145732
